TPU v7x, 512 devices: a whole 4x8x8 slice. The times are simulated.
512 devices in a mesh: ctx: 64 (over y, x, core), head: 8 (over z).
Axes of the slice: x: 4, y: 8, z: 8, core: 2. Of those that a mesh axis runs over, the one named last changes fastest.
Arguments:
- tokens: bfloat16 [65536, 2048], P('ctx', 'head'), may hold values from -6 to 6
- w_qkv: bfloat16 [3, 2048, 2048], P(None, 'ctx', 'head'), may hold values from -0.125 to 0.125
- out_gain: float32 [2048], P('head'), may hold values from 0.25 to 1.75
- seg_ids: int32 [65536], P('ctx'), may hold values from 0 to 15, never falling along the last dimension, each value on 1 to 16384 neighbouring positions
Outputs:
- attended: bfloat16 [65536, 2048], P('ctx', 'head')
Inputs may be any that keep to these rules, and one draw needn't show every extreme that they name: `seg_ids`: segment numbers never fall along the stream; each segment covers 1 to 16384 consecutive tokens, and one covers exactly 16384.
All inputs are finite; a program needn't handle non-finite values.
Results may differ from a plain program's by a relative error of at most 0.012.
Values may be sent and summed in bfloat16 or wider, within the bound.
No kernel may reach another device: no remote copies, remote signals or barrier semaphores. Data moves between devices by JAX's collectives and lax.ppermute only.
A program may use at most 64 MiB of HBM per device.

v0:
```python
import jax
import jax.numpy as jnp
from jax import lax
from jax.sharding import PartitionSpec as P

HEAD_DIM = 128


def passed_along(value, axis, steps):
    count = lax.axis_size(axis)
    leading, last = (max(0, -steps), min(count, count - steps))
    return lax.ppermute(value, axis, [(source, source + steps) for source in range(leading, last)])


def feature_map(values):
    return (jax.nn.elu(values.astype(jnp.float32)) + 1.0).astype(jnp.bfloat16)


def combine(earlier, later):
    first_state, first_tail = earlier
    later_state, later_tail = later
    linked = (first_tail == later_tail) | (later_tail < 0.0)
    return (
        later_state + jnp.where(linked, first_state, 0.0),
        jnp.where(later_tail < 0.0, first_tail, later_tail),
    )


def prepare(projected, segment):
    row_count = segment.shape[0]
    head_count = projected.shape[2] // HEAD_DIM
    queries = feature_map(projected[0]).reshape(row_count, head_count, HEAD_DIM)
    key_map = feature_map(projected[1]).reshape(row_count, head_count, HEAD_DIM)
    values = projected[2].reshape(row_count, head_count, HEAD_DIM)
    seg_float = segment.astype(jnp.float32)
    tail_id = seg_float[-1]
    key_tail = jnp.where((seg_float == tail_id)[:, None, None], key_map, jnp.zeros_like(key_map))
    kv_state = jnp.einsum("thd,the->hde", key_tail, values, preferred_element_type=jnp.float32)
    return (queries, key_map, values, seg_float, kv_state, tail_id)


def complete(queries, key_map, values, seg_float, state_in, tail_in, out_gain):
    row_count, head_count = (queries.shape[0], queries.shape[1])
    state_low = state_in.astype(jnp.bfloat16)
    prefix = jnp.einsum("thd,hde->the", queries, state_low, preferred_element_type=jnp.float32)
    prefix = jnp.where((seg_float == tail_in)[:, None, None], prefix, 0.0)
    block_rows = min(512, row_count)
    positions = jnp.arange(row_count, dtype=jnp.int32)

    def one_block(blk_no):
        first_row = blk_no * block_rows
        query_blk = lax.dynamic_slice_in_dim(queries, first_row, block_rows, 0)
        query_pos = first_row + jnp.arange(block_rows, dtype=jnp.int32)
        query_seg = lax.dynamic_slice_in_dim(seg_float, first_row, block_rows, 0)
        scores = jnp.einsum("bhd,shd->hbs", query_blk, key_map, preferred_element_type=jnp.float32)
        visible = (positions[None, :] <= query_pos[:, None]) & (
            seg_float[None, :] == query_seg[:, None]
        )
        weights = jnp.where(visible[None], scores, 0.0).astype(jnp.bfloat16)
        return jnp.einsum("hbs,she->bhe", weights, values, preferred_element_type=jnp.float32)

    local_part = lax.map(one_block, jnp.arange(row_count // block_rows, dtype=jnp.int32))
    numerator = local_part.reshape(row_count, head_count, HEAD_DIM) + prefix
    inv_norm = lax.rsqrt(jnp.mean(numerator * numerator, axis=-1, keepdims=True) + 1e-05)
    result = numerator * inv_norm * out_gain.reshape(head_count, HEAD_DIM)
    return result.astype(jnp.bfloat16).reshape(row_count, head_count * HEAD_DIM)


def per_device(tokens, w_qkv, out_gain, seg_ids):
    whole = lax.all_gather(tokens, "head", axis=1, tiled=True)
    projected = jnp.einsum(
        "tr,grc->gtc",
        whole,
        lax.all_gather(w_qkv, "ctx", axis=1, tiled=True),
        preferred_element_type=jnp.float32,
    ).astype(jnp.bfloat16)
    queries, key_map, values, seg_float, kv_state, tail_id = prepare(projected, seg_ids)
    empty_state = jnp.zeros_like(kv_state)
    own_pair = (kv_state, tail_id)

    def hand_round(turn_no, carried):
        running, _ = carried
        incoming = (
            passed_along(running[0].astype(jnp.bfloat16), "ctx", 1).astype(jnp.float32),
            passed_along(running[1].astype(jnp.bfloat16), "ctx", 1).astype(jnp.float32),
        )
        return (combine(incoming, own_pair), incoming)

    start_pair = (empty_state, jnp.array(-1.0, jnp.float32))
    _, arrived = lax.fori_loop(0, lax.axis_size("ctx") - 1, hand_round, (own_pair, start_pair))
    state_in, tail_in = arrived
    return complete(queries, key_map, values, seg_float, state_in, tail_in, out_gain)


def solution(mesh):
    placed = (P("ctx", "head"), P(None, "ctx", "head"), P("head"), P("ctx"))
    return jax.shard_map(
        per_device, mesh=mesh, in_specs=placed, out_specs=P("ctx", "head"), check_vma=False
    )
```

profile of v0, /device:TPU:32, one launch (start us, length us, event | category | flops | bytes accessed | tf_op | source)
XLA Modules:
  0.0 1084.5 jit_solution(1804793181118891656)
XLA Ops:
  12.1 84.4 %all-gather.3.cloned.1.call-done = bf16[3,2048,256]{2,1,0:T(8,128)(2,1)} async-done(((bf16[3,32,256]{2,1,0:T(8,128)(2,1)}), bf16[3,2048,256]{2,1,0:T(8,128)(2,1)}) %all-gather.3.cloned.1.call-update) | async-done | bytes 3145744 | tf_op jit(solution)/shard_map/all_gather | solution.py:74
  96.5 67.6 %all-gather.5.cloned.1.call-done = bf16[1024,2048]{1,0:T(8,128)(2,1)} async-done(((bf16[1024,256]{1,0:T(8,128)(2,1)}), bf16[1024,2048]{1,0:T(8,128)(2,1)}) %all-gather.5.cloned.1.call-update) | async-done | bytes 4194320 | tf_op jit(solution)/shard_map/all_gather | solution.py:70
  164.0 6.6 fusion.15
  176.5 877.2 %while.28 = (s32[]{:T(128)}, bf16[2,128,128]{2,1,0:T(8,128)(2,1)S(1)}, bf16[]{:T(256)}, bf16[2,128,128]{2,1,0:T(8,128)(2,1)}, f32[]{:T(128)}, /*index=5*/f32[]{:...) while((s32[]{:T(128)}, bf16[2,128,128]{2,1,0:T(8,128)(2,1)S(1)}, bf16[]{:T(256)}, ...), condition=%wide.region_3.4_spmd, body=%wide.region_2.3_spmd.sunk | while | flops 163846 | bytes 590031 | solution.py:90
  195.3 5.4 collective-permute-done
  209.2 5.4 collective-permute-done
  223.1 5.4 collective-permute-done
  237.0 5.4 collective-permute-done
  250.9 5.4 collective-permute-done
  264.9 5.4 collective-permute-done
  278.8 5.4 collective-permute-done
  292.7 5.4 collective-permute-done
  306.6 5.4 collective-permute-done
  320.6 5.4 collective-permute-done
  334.5 5.4 collective-permute-done
  348.4 5.4 collective-permute-done
  362.3 5.4 collective-permute-done
  376.3 5.4 collective-permute-done
  390.2 5.4 collective-permute-done
  404.1 5.4 collective-permute-done
  418.0 5.4 collective-permute-done
  432.0 5.4 collective-permute-done
  445.9 5.4 collective-permute-done
  459.8 5.4 collective-permute-done
  473.7 5.4 collective-permute-done
  487.6 5.4 collective-permute-done
  501.6 5.4 collective-permute-done
  515.5 5.4 collective-permute-done
  529.4 5.4 collective-permute-done
  543.3 5.4 collective-permute-done
  557.3 5.4 collective-permute-done
  571.2 5.4 collective-permute-done
  585.1 5.4 collective-permute-done
  599.0 5.4 collective-permute-done
  613.0 5.4 collective-permute-done
  626.9 5.4 collective-permute-done
  640.8 5.4 collective-permute-done
  654.7 5.4 collective-permute-done
  668.6 5.4 collective-permute-done
  682.6 5.4 collective-permute-done
  696.5 5.4 collective-permute-done
  710.4 5.4 collective-permute-done
  724.3 5.4 collective-permute-done
  738.3 5.4 collective-permute-done
  752.2 5.4 collective-permute-done
  766.1 5.4 collective-permute-done
  780.0 5.4 collective-permute-done
  794.0 5.4 collective-permute-done
  807.9 5.4 collective-permute-done
  821.8 5.4 collective-permute-done
  835.7 5.4 collective-permute-done
  849.6 5.4 collective-permute-done
  863.6 5.4 collective-permute-done
  877.5 5.4 collective-permute-done
  891.4 5.4 collective-permute-done
  905.3 5.4 collective-permute-done
  933.2 5.4 collective-permute-done
  947.1 5.4 collective-permute-done
  961.0 5.4 collective-permute-done
  975.0 5.4 collective-permute-done
  988.9 5.4 collective-permute-done
  1002.8 5.4 collective-permute-done
  1016.7 5.4 collective-permute-done
  1056.0 19.2 %while.29 = (s32[]{:T(128)}, f32[2,512,2,128]{1,0,3,2:T(2,128)S(1)}, s32[2]{0:T(128)S(1)}, f32[1024]{0:T(1024)S(1)}, bf16[1024,2,128]{2,1,0:T(2,128)(2,1)S(1)}, ...) while((s32[]{:T(128)}, ...), condition=%wide.region_1.2_spmd.clone, body=%wide.region_0.1_spmd.clone.sunk | while | flops 540541440 | bytes 5519551 | solution.py:62
  (303 shorter events, 395.1 us)
Async XLA Ops:
  6.5 89.9 %all-gather.3.cloned.1.call-start = ((), (), s32[]{:S(2)}) async-start(), calls=%async_computation | async-start | bytes 3194880 | tf_op jit(solution)/shard_map/all_gather | solution.py:74
  7.3 156.8 %all-gather.5.cloned.1.call-start = ((), (), s32[]{:S(2)}) async-start(), calls=%async_computation.1 | async-start | bytes 4718592 | tf_op jit(solution)/shard_map/all_gather | solution.py:70
  176.5 13.3 %collective-permute-start.1 = (bf16[2,128,128]{2,1,0:T(8,128)(2,1)S(1)}, bf16[2,128,128]{2,1,0:T(8,128)(2,1)S(1)}, u32[]{:S(2)}, u32[]{:S(2)}) collective-permute-start(bf16[2,128,128]{2,1,0:T(8,128)(2,1)S(1)} %get-tuple-element.318), channel_id=1, source_target_pairs={{0,8},{8,16},{16,24},{24,32},{32,40},{40,48},{48,56},{56,64},{64,7... | collective-permute-start | bytes 196616 | tf_op jit(solution)/shard_map/while/body/eval_jaxpr/ppermute | solution.py:12
  190.5 13.3 %collective-permute-start.1 = (bf16[2,128,128]{2,1,0:T(8,128)(2,1)S(1)}, bf16[2,128,128]{2,1,0:T(8,128)(2,1)S(1)}, u32[]{:S(2)}, u32[]{:S(2)}) collective-permute-start(bf16[2,128,128]{2,1,0:T(8,128)(2,1)S(1)} %get-tuple-element.318), channel_id=1, source_target_pairs={{0,8},{8,16},{16,24},{24,32},{32,40},{40,48},{48,56},{56,64},{64,7... | collective-permute-start | bytes 196616 | tf_op jit(solution)/shard_map/while/body/eval_jaxpr/ppermute | solution.py:12
  204.4 13.3 %collective-permute-start.1 = (bf16[2,128,128]{2,1,0:T(8,128)(2,1)S(1)}, bf16[2,128,128]{2,1,0:T(8,128)(2,1)S(1)}, u32[]{:S(2)}, u32[]{:S(2)}) collective-permute-start(bf16[2,128,128]{2,1,0:T(8,128)(2,1)S(1)} %get-tuple-element.318), channel_id=1, source_target_pairs={{0,8},{8,16},{16,24},{24,32},{32,40},{40,48},{48,56},{56,64},{64,7... | collective-permute-start | bytes 196616 | tf_op jit(solution)/shard_map/while/body/eval_jaxpr/ppermute | solution.py:12
  218.3 13.3 %collective-permute-start.1 = (bf16[2,128,128]{2,1,0:T(8,128)(2,1)S(1)}, bf16[2,128,128]{2,1,0:T(8,128)(2,1)S(1)}, u32[]{:S(2)}, u32[]{:S(2)}) collective-permute-start(bf16[2,128,128]{2,1,0:T(8,128)(2,1)S(1)} %get-tuple-element.318), channel_id=1, source_target_pairs={{0,8},{8,16},{16,24},{24,32},{32,40},{40,48},{48,56},{56,64},{64,7... | collective-permute-start | bytes 196616 | tf_op jit(solution)/shard_map/while/body/eval_jaxpr/ppermute | solution.py:12
  232.3 13.3 %collective-permute-start.1 = (bf16[2,128,128]{2,1,0:T(8,128)(2,1)S(1)}, bf16[2,128,128]{2,1,0:T(8,128)(2,1)S(1)}, u32[]{:S(2)}, u32[]{:S(2)}) collective-permute-start(bf16[2,128,128]{2,1,0:T(8,128)(2,1)S(1)} %get-tuple-element.318), channel_id=1, source_target_pairs={{0,8},{8,16},{16,24},{24,32},{32,40},{40,48},{48,56},{56,64},{64,7... | collective-permute-start | bytes 196616 | tf_op jit(solution)/shard_map/while/body/eval_jaxpr/ppermute | solution.py:12
  246.2 13.3 %collective-permute-start.1 = (bf16[2,128,128]{2,1,0:T(8,128)(2,1)S(1)}, bf16[2,128,128]{2,1,0:T(8,128)(2,1)S(1)}, u32[]{:S(2)}, u32[]{:S(2)}) collective-permute-start(bf16[2,128,128]{2,1,0:T(8,128)(2,1)S(1)} %get-tuple-element.318), channel_id=1, source_target_pairs={{0,8},{8,16},{16,24},{24,32},{32,40},{40,48},{48,56},{56,64},{64,7... | collective-permute-start | bytes 196616 | tf_op jit(solution)/shard_map/while/body/eval_jaxpr/ppermute | solution.py:12
  260.1 13.3 %collective-permute-start.1 = (bf16[2,128,128]{2,1,0:T(8,128)(2,1)S(1)}, bf16[2,128,128]{2,1,0:T(8,128)(2,1)S(1)}, u32[]{:S(2)}, u32[]{:S(2)}) collective-permute-start(bf16[2,128,128]{2,1,0:T(8,128)(2,1)S(1)} %get-tuple-element.318), channel_id=1, source_target_pairs={{0,8},{8,16},{16,24},{24,32},{32,40},{40,48},{48,56},{56,64},{64,7... | collective-permute-start | bytes 196616 | tf_op jit(solution)/shard_map/while/body/eval_jaxpr/ppermute | solution.py:12
  274.0 13.3 %collective-permute-start.1 = (bf16[2,128,128]{2,1,0:T(8,128)(2,1)S(1)}, bf16[2,128,128]{2,1,0:T(8,128)(2,1)S(1)}, u32[]{:S(2)}, u32[]{:S(2)}) collective-permute-start(bf16[2,128,128]{2,1,0:T(8,128)(2,1)S(1)} %get-tuple-element.318), channel_id=1, source_target_pairs={{0,8},{8,16},{16,24},{24,32},{32,40},{40,48},{48,56},{56,64},{64,7... | collective-permute-start | bytes 196616 | tf_op jit(solution)/shard_map/while/body/eval_jaxpr/ppermute | solution.py:12
  287.9 13.3 %collective-permute-start.1 = (bf16[2,128,128]{2,1,0:T(8,128)(2,1)S(1)}, bf16[2,128,128]{2,1,0:T(8,128)(2,1)S(1)}, u32[]{:S(2)}, u32[]{:S(2)}) collective-permute-start(bf16[2,128,128]{2,1,0:T(8,128)(2,1)S(1)} %get-tuple-element.318), channel_id=1, source_target_pairs={{0,8},{8,16},{16,24},{24,32},{32,40},{40,48},{48,56},{56,64},{64,7... | collective-permute-start | bytes 196616 | tf_op jit(solution)/shard_map/while/body/eval_jaxpr/ppermute | solution.py:12
  301.9 13.3 %collective-permute-start.1 = (bf16[2,128,128]{2,1,0:T(8,128)(2,1)S(1)}, bf16[2,128,128]{2,1,0:T(8,128)(2,1)S(1)}, u32[]{:S(2)}, u32[]{:S(2)}) collective-permute-start(bf16[2,128,128]{2,1,0:T(8,128)(2,1)S(1)} %get-tuple-element.318), channel_id=1, source_target_pairs={{0,8},{8,16},{16,24},{24,32},{32,40},{40,48},{48,56},{56,64},{64,7... | collective-permute-start | bytes 196616 | tf_op jit(solution)/shard_map/while/body/eval_jaxpr/ppermute | solution.py:12
  315.8 13.3 %collective-permute-start.1 = (bf16[2,128,128]{2,1,0:T(8,128)(2,1)S(1)}, bf16[2,128,128]{2,1,0:T(8,128)(2,1)S(1)}, u32[]{:S(2)}, u32[]{:S(2)}) collective-permute-start(bf16[2,128,128]{2,1,0:T(8,128)(2,1)S(1)} %get-tuple-element.318), channel_id=1, source_target_pairs={{0,8},{8,16},{16,24},{24,32},{32,40},{40,48},{48,56},{56,64},{64,7... | collective-permute-start | bytes 196616 | tf_op jit(solution)/shard_map/while/body/eval_jaxpr/ppermute | solution.py:12
  329.7 13.3 %collective-permute-start.1 = (bf16[2,128,128]{2,1,0:T(8,128)(2,1)S(1)}, bf16[2,128,128]{2,1,0:T(8,128)(2,1)S(1)}, u32[]{:S(2)}, u32[]{:S(2)}) collective-permute-start(bf16[2,128,128]{2,1,0:T(8,128)(2,1)S(1)} %get-tuple-element.318), channel_id=1, source_target_pairs={{0,8},{8,16},{16,24},{24,32},{32,40},{40,48},{48,56},{56,64},{64,7... | collective-permute-start | bytes 196616 | tf_op jit(solution)/shard_map/while/body/eval_jaxpr/ppermute | solution.py:12
  343.6 13.3 %collective-permute-start.1 = (bf16[2,128,128]{2,1,0:T(8,128)(2,1)S(1)}, bf16[2,128,128]{2,1,0:T(8,128)(2,1)S(1)}, u32[]{:S(2)}, u32[]{:S(2)}) collective-permute-start(bf16[2,128,128]{2,1,0:T(8,128)(2,1)S(1)} %get-tuple-element.318), channel_id=1, source_target_pairs={{0,8},{8,16},{16,24},{24,32},{32,40},{40,48},{48,56},{56,64},{64,7... | collective-permute-start | bytes 196616 | tf_op jit(solution)/shard_map/while/body/eval_jaxpr/ppermute | solution.py:12
  357.6 13.3 %collective-permute-start.1 = (bf16[2,128,128]{2,1,0:T(8,128)(2,1)S(1)}, bf16[2,128,128]{2,1,0:T(8,128)(2,1)S(1)}, u32[]{:S(2)}, u32[]{:S(2)}) collective-permute-start(bf16[2,128,128]{2,1,0:T(8,128)(2,1)S(1)} %get-tuple-element.318), channel_id=1, source_target_pairs={{0,8},{8,16},{16,24},{24,32},{32,40},{40,48},{48,56},{56,64},{64,7... | collective-permute-start | bytes 196616 | tf_op jit(solution)/shard_map/while/body/eval_jaxpr/ppermute | solution.py:12
  371.5 13.3 %collective-permute-start.1 = (bf16[2,128,128]{2,1,0:T(8,128)(2,1)S(1)}, bf16[2,128,128]{2,1,0:T(8,128)(2,1)S(1)}, u32[]{:S(2)}, u32[]{:S(2)}) collective-permute-start(bf16[2,128,128]{2,1,0:T(8,128)(2,1)S(1)} %get-tuple-element.318), channel_id=1, source_target_pairs={{0,8},{8,16},{16,24},{24,32},{32,40},{40,48},{48,56},{56,64},{64,7... | collective-permute-start | bytes 196616 | tf_op jit(solution)/shard_map/while/body/eval_jaxpr/ppermute | solution.py:12
  385.4 13.3 %collective-permute-start.1 = (bf16[2,128,128]{2,1,0:T(8,128)(2,1)S(1)}, bf16[2,128,128]{2,1,0:T(8,128)(2,1)S(1)}, u32[]{:S(2)}, u32[]{:S(2)}) collective-permute-start(bf16[2,128,128]{2,1,0:T(8,128)(2,1)S(1)} %get-tuple-element.318), channel_id=1, source_target_pairs={{0,8},{8,16},{16,24},{24,32},{32,40},{40,48},{48,56},{56,64},{64,7... | collective-permute-start | bytes 196616 | tf_op jit(solution)/shard_map/while/body/eval_jaxpr/ppermute | solution.py:12
  399.3 13.3 %collective-permute-start.1 = (bf16[2,128,128]{2,1,0:T(8,128)(2,1)S(1)}, bf16[2,128,128]{2,1,0:T(8,128)(2,1)S(1)}, u32[]{:S(2)}, u32[]{:S(2)}) collective-permute-start(bf16[2,128,128]{2,1,0:T(8,128)(2,1)S(1)} %get-tuple-element.318), channel_id=1, source_target_pairs={{0,8},{8,16},{16,24},{24,32},{32,40},{40,48},{48,56},{56,64},{64,7... | collective-permute-start | bytes 196616 | tf_op jit(solution)/shard_map/while/body/eval_jaxpr/ppermute | solution.py:12
  413.3 13.3 %collective-permute-start.1 = (bf16[2,128,128]{2,1,0:T(8,128)(2,1)S(1)}, bf16[2,128,128]{2,1,0:T(8,128)(2,1)S(1)}, u32[]{:S(2)}, u32[]{:S(2)}) collective-permute-start(bf16[2,128,128]{2,1,0:T(8,128)(2,1)S(1)} %get-tuple-element.318), channel_id=1, source_target_pairs={{0,8},{8,16},{16,24},{24,32},{32,40},{40,48},{48,56},{56,64},{64,7... | collective-permute-start | bytes 196616 | tf_op jit(solution)/shard_map/while/body/eval_jaxpr/ppermute | solution.py:12
  427.2 13.3 %collective-permute-start.1 = (bf16[2,128,128]{2,1,0:T(8,128)(2,1)S(1)}, bf16[2,128,128]{2,1,0:T(8,128)(2,1)S(1)}, u32[]{:S(2)}, u32[]{:S(2)}) collective-permute-start(bf16[2,128,128]{2,1,0:T(8,128)(2,1)S(1)} %get-tuple-element.318), channel_id=1, source_target_pairs={{0,8},{8,16},{16,24},{24,32},{32,40},{40,48},{48,56},{56,64},{64,7... | collective-permute-start | bytes 196616 | tf_op jit(solution)/shard_map/while/body/eval_jaxpr/ppermute | solution.py:12
  441.1 13.3 %collective-permute-start.1 = (bf16[2,128,128]{2,1,0:T(8,128)(2,1)S(1)}, bf16[2,128,128]{2,1,0:T(8,128)(2,1)S(1)}, u32[]{:S(2)}, u32[]{:S(2)}) collective-permute-start(bf16[2,128,128]{2,1,0:T(8,128)(2,1)S(1)} %get-tuple-element.318), channel_id=1, source_target_pairs={{0,8},{8,16},{16,24},{24,32},{32,40},{40,48},{48,56},{56,64},{64,7... | collective-permute-start | bytes 196616 | tf_op jit(solution)/shard_map/while/body/eval_jaxpr/ppermute | solution.py:12
  455.0 13.3 %collective-permute-start.1 = (bf16[2,128,128]{2,1,0:T(8,128)(2,1)S(1)}, bf16[2,128,128]{2,1,0:T(8,128)(2,1)S(1)}, u32[]{:S(2)}, u32[]{:S(2)}) collective-permute-start(bf16[2,128,128]{2,1,0:T(8,128)(2,1)S(1)} %get-tuple-element.318), channel_id=1, source_target_pairs={{0,8},{8,16},{16,24},{24,32},{32,40},{40,48},{48,56},{56,64},{64,7... | collective-permute-start | bytes 196616 | tf_op jit(solution)/shard_map/while/body/eval_jaxpr/ppermute | solution.py:12
  468.9 13.3 %collective-permute-start.1 = (bf16[2,128,128]{2,1,0:T(8,128)(2,1)S(1)}, bf16[2,128,128]{2,1,0:T(8,128)(2,1)S(1)}, u32[]{:S(2)}, u32[]{:S(2)}) collective-permute-start(bf16[2,128,128]{2,1,0:T(8,128)(2,1)S(1)} %get-tuple-element.318), channel_id=1, source_target_pairs={{0,8},{8,16},{16,24},{24,32},{32,40},{40,48},{48,56},{56,64},{64,7... | collective-permute-start | bytes 196616 | tf_op jit(solution)/shard_map/while/body/eval_jaxpr/ppermute | solution.py:12
  482.9 13.3 %collective-permute-start.1 = (bf16[2,128,128]{2,1,0:T(8,128)(2,1)S(1)}, bf16[2,128,128]{2,1,0:T(8,128)(2,1)S(1)}, u32[]{:S(2)}, u32[]{:S(2)}) collective-permute-start(bf16[2,128,128]{2,1,0:T(8,128)(2,1)S(1)} %get-tuple-element.318), channel_id=1, source_target_pairs={{0,8},{8,16},{16,24},{24,32},{32,40},{40,48},{48,56},{56,64},{64,7... | collective-permute-start | bytes 196616 | tf_op jit(solution)/shard_map/while/body/eval_jaxpr/ppermute | solution.py:12
  496.8 13.3 %collective-permute-start.1 = (bf16[2,128,128]{2,1,0:T(8,128)(2,1)S(1)}, bf16[2,128,128]{2,1,0:T(8,128)(2,1)S(1)}, u32[]{:S(2)}, u32[]{:S(2)}) collective-permute-start(bf16[2,128,128]{2,1,0:T(8,128)(2,1)S(1)} %get-tuple-element.318), channel_id=1, source_target_pairs={{0,8},{8,16},{16,24},{24,32},{32,40},{40,48},{48,56},{56,64},{64,7... | collective-permute-start | bytes 196616 | tf_op jit(solution)/shard_map/while/body/eval_jaxpr/ppermute | solution.py:12
  510.7 13.3 %collective-permute-start.1 = (bf16[2,128,128]{2,1,0:T(8,128)(2,1)S(1)}, bf16[2,128,128]{2,1,0:T(8,128)(2,1)S(1)}, u32[]{:S(2)}, u32[]{:S(2)}) collective-permute-start(bf16[2,128,128]{2,1,0:T(8,128)(2,1)S(1)} %get-tuple-element.318), channel_id=1, source_target_pairs={{0,8},{8,16},{16,24},{24,32},{32,40},{40,48},{48,56},{56,64},{64,7... | collective-permute-start | bytes 196616 | tf_op jit(solution)/shard_map/while/body/eval_jaxpr/ppermute | solution.py:12
  524.6 13.3 %collective-permute-start.1 = (bf16[2,128,128]{2,1,0:T(8,128)(2,1)S(1)}, bf16[2,128,128]{2,1,0:T(8,128)(2,1)S(1)}, u32[]{:S(2)}, u32[]{:S(2)}) collective-permute-start(bf16[2,128,128]{2,1,0:T(8,128)(2,1)S(1)} %get-tuple-element.318), channel_id=1, source_target_pairs={{0,8},{8,16},{16,24},{24,32},{32,40},{40,48},{48,56},{56,64},{64,7... | collective-permute-start | bytes 196616 | tf_op jit(solution)/shard_map/while/body/eval_jaxpr/ppermute | solution.py:12
  538.6 13.3 %collective-permute-start.1 = (bf16[2,128,128]{2,1,0:T(8,128)(2,1)S(1)}, bf16[2,128,128]{2,1,0:T(8,128)(2,1)S(1)}, u32[]{:S(2)}, u32[]{:S(2)}) collective-permute-start(bf16[2,128,128]{2,1,0:T(8,128)(2,1)S(1)} %get-tuple-element.318), channel_id=1, source_target_pairs={{0,8},{8,16},{16,24},{24,32},{32,40},{40,48},{48,56},{56,64},{64,7... | collective-permute-start | bytes 196616 | tf_op jit(solution)/shard_map/while/body/eval_jaxpr/ppermute | solution.py:12
  552.5 13.3 %collective-permute-start.1 = (bf16[2,128,128]{2,1,0:T(8,128)(2,1)S(1)}, bf16[2,128,128]{2,1,0:T(8,128)(2,1)S(1)}, u32[]{:S(2)}, u32[]{:S(2)}) collective-permute-start(bf16[2,128,128]{2,1,0:T(8,128)(2,1)S(1)} %get-tuple-element.318), channel_id=1, source_target_pairs={{0,8},{8,16},{16,24},{24,32},{32,40},{40,48},{48,56},{56,64},{64,7... | collective-permute-start | bytes 196616 | tf_op jit(solution)/shard_map/while/body/eval_jaxpr/ppermute | solution.py:12
  566.4 13.3 %collective-permute-start.1 = (bf16[2,128,128]{2,1,0:T(8,128)(2,1)S(1)}, bf16[2,128,128]{2,1,0:T(8,128)(2,1)S(1)}, u32[]{:S(2)}, u32[]{:S(2)}) collective-permute-start(bf16[2,128,128]{2,1,0:T(8,128)(2,1)S(1)} %get-tuple-element.318), channel_id=1, source_target_pairs={{0,8},{8,16},{16,24},{24,32},{32,40},{40,48},{48,56},{56,64},{64,7... | collective-permute-start | bytes 196616 | tf_op jit(solution)/shard_map/while/body/eval_jaxpr/ppermute | solution.py:12
  580.3 13.3 %collective-permute-start.1 = (bf16[2,128,128]{2,1,0:T(8,128)(2,1)S(1)}, bf16[2,128,128]{2,1,0:T(8,128)(2,1)S(1)}, u32[]{:S(2)}, u32[]{:S(2)}) collective-permute-start(bf16[2,128,128]{2,1,0:T(8,128)(2,1)S(1)} %get-tuple-element.318), channel_id=1, source_target_pairs={{0,8},{8,16},{16,24},{24,32},{32,40},{40,48},{48,56},{56,64},{64,7... | collective-permute-start | bytes 196616 | tf_op jit(solution)/shard_map/while/body/eval_jaxpr/ppermute | solution.py:12
  594.3 13.3 %collective-permute-start.1 = (bf16[2,128,128]{2,1,0:T(8,128)(2,1)S(1)}, bf16[2,128,128]{2,1,0:T(8,128)(2,1)S(1)}, u32[]{:S(2)}, u32[]{:S(2)}) collective-permute-start(bf16[2,128,128]{2,1,0:T(8,128)(2,1)S(1)} %get-tuple-element.318), channel_id=1, source_target_pairs={{0,8},{8,16},{16,24},{24,32},{32,40},{40,48},{48,56},{56,64},{64,7... | collective-permute-start | bytes 196616 | tf_op jit(solution)/shard_map/while/body/eval_jaxpr/ppermute | solution.py:12
  608.2 13.3 %collective-permute-start.1 = (bf16[2,128,128]{2,1,0:T(8,128)(2,1)S(1)}, bf16[2,128,128]{2,1,0:T(8,128)(2,1)S(1)}, u32[]{:S(2)}, u32[]{:S(2)}) collective-permute-start(bf16[2,128,128]{2,1,0:T(8,128)(2,1)S(1)} %get-tuple-element.318), channel_id=1, source_target_pairs={{0,8},{8,16},{16,24},{24,32},{32,40},{40,48},{48,56},{56,64},{64,7... | collective-permute-start | bytes 196616 | tf_op jit(solution)/shard_map/while/body/eval_jaxpr/ppermute | solution.py:12
  622.1 13.3 %collective-permute-start.1 = (bf16[2,128,128]{2,1,0:T(8,128)(2,1)S(1)}, bf16[2,128,128]{2,1,0:T(8,128)(2,1)S(1)}, u32[]{:S(2)}, u32[]{:S(2)}) collective-permute-start(bf16[2,128,128]{2,1,0:T(8,128)(2,1)S(1)} %get-tuple-element.318), channel_id=1, source_target_pairs={{0,8},{8,16},{16,24},{24,32},{32,40},{40,48},{48,56},{56,64},{64,7... | collective-permute-start | bytes 196616 | tf_op jit(solution)/shard_map/while/body/eval_jaxpr/ppermute | solution.py:12
  636.0 13.3 %collective-permute-start.1 = (bf16[2,128,128]{2,1,0:T(8,128)(2,1)S(1)}, bf16[2,128,128]{2,1,0:T(8,128)(2,1)S(1)}, u32[]{:S(2)}, u32[]{:S(2)}) collective-permute-start(bf16[2,128,128]{2,1,0:T(8,128)(2,1)S(1)} %get-tuple-element.318), channel_id=1, source_target_pairs={{0,8},{8,16},{16,24},{24,32},{32,40},{40,48},{48,56},{56,64},{64,7... | collective-permute-start | bytes 196616 | tf_op jit(solution)/shard_map/while/body/eval_jaxpr/ppermute | solution.py:12
  649.9 13.3 %collective-permute-start.1 = (bf16[2,128,128]{2,1,0:T(8,128)(2,1)S(1)}, bf16[2,128,128]{2,1,0:T(8,128)(2,1)S(1)}, u32[]{:S(2)}, u32[]{:S(2)}) collective-permute-start(bf16[2,128,128]{2,1,0:T(8,128)(2,1)S(1)} %get-tuple-element.318), channel_id=1, source_target_pairs={{0,8},{8,16},{16,24},{24,32},{32,40},{40,48},{48,56},{56,64},{64,7... | collective-permute-start | bytes 196616 | tf_op jit(solution)/shard_map/while/body/eval_jaxpr/ppermute | solution.py:12
  663.9 13.3 %collective-permute-start.1 = (bf16[2,128,128]{2,1,0:T(8,128)(2,1)S(1)}, bf16[2,128,128]{2,1,0:T(8,128)(2,1)S(1)}, u32[]{:S(2)}, u32[]{:S(2)}) collective-permute-start(bf16[2,128,128]{2,1,0:T(8,128)(2,1)S(1)} %get-tuple-element.318), channel_id=1, source_target_pairs={{0,8},{8,16},{16,24},{24,32},{32,40},{40,48},{48,56},{56,64},{64,7... | collective-permute-start | bytes 196616 | tf_op jit(solution)/shard_map/while/body/eval_jaxpr/ppermute | solution.py:12
  677.8 13.3 %collective-permute-start.1 = (bf16[2,128,128]{2,1,0:T(8,128)(2,1)S(1)}, bf16[2,128,128]{2,1,0:T(8,128)(2,1)S(1)}, u32[]{:S(2)}, u32[]{:S(2)}) collective-permute-start(bf16[2,128,128]{2,1,0:T(8,128)(2,1)S(1)} %get-tuple-element.318), channel_id=1, source_target_pairs={{0,8},{8,16},{16,24},{24,32},{32,40},{40,48},{48,56},{56,64},{64,7... | collective-permute-start | bytes 196616 | tf_op jit(solution)/shard_map/while/body/eval_jaxpr/ppermute | solution.py:12
  691.7 13.3 %collective-permute-start.1 = (bf16[2,128,128]{2,1,0:T(8,128)(2,1)S(1)}, bf16[2,128,128]{2,1,0:T(8,128)(2,1)S(1)}, u32[]{:S(2)}, u32[]{:S(2)}) collective-permute-start(bf16[2,128,128]{2,1,0:T(8,128)(2,1)S(1)} %get-tuple-element.318), channel_id=1, source_target_pairs={{0,8},{8,16},{16,24},{24,32},{32,40},{40,48},{48,56},{56,64},{64,7... | collective-permute-start | bytes 196616 | tf_op jit(solution)/shard_map/while/body/eval_jaxpr/ppermute | solution.py:12
  705.6 13.3 %collective-permute-start.1 = (bf16[2,128,128]{2,1,0:T(8,128)(2,1)S(1)}, bf16[2,128,128]{2,1,0:T(8,128)(2,1)S(1)}, u32[]{:S(2)}, u32[]{:S(2)}) collective-permute-start(bf16[2,128,128]{2,1,0:T(8,128)(2,1)S(1)} %get-tuple-element.318), channel_id=1, source_target_pairs={{0,8},{8,16},{16,24},{24,32},{32,40},{40,48},{48,56},{56,64},{64,7... | collective-permute-start | bytes 196616 | tf_op jit(solution)/shard_map/while/body/eval_jaxpr/ppermute | solution.py:12
  719.6 13.3 %collective-permute-start.1 = (bf16[2,128,128]{2,1,0:T(8,128)(2,1)S(1)}, bf16[2,128,128]{2,1,0:T(8,128)(2,1)S(1)}, u32[]{:S(2)}, u32[]{:S(2)}) collective-permute-start(bf16[2,128,128]{2,1,0:T(8,128)(2,1)S(1)} %get-tuple-element.318), channel_id=1, source_target_pairs={{0,8},{8,16},{16,24},{24,32},{32,40},{40,48},{48,56},{56,64},{64,7... | collective-permute-start | bytes 196616 | tf_op jit(solution)/shard_map/while/body/eval_jaxpr/ppermute | solution.py:12
  733.5 13.3 %collective-permute-start.1 = (bf16[2,128,128]{2,1,0:T(8,128)(2,1)S(1)}, bf16[2,128,128]{2,1,0:T(8,128)(2,1)S(1)}, u32[]{:S(2)}, u32[]{:S(2)}) collective-permute-start(bf16[2,128,128]{2,1,0:T(8,128)(2,1)S(1)} %get-tuple-element.318), channel_id=1, source_target_pairs={{0,8},{8,16},{16,24},{24,32},{32,40},{40,48},{48,56},{56,64},{64,7... | collective-permute-start | bytes 196616 | tf_op jit(solution)/shard_map/while/body/eval_jaxpr/ppermute | solution.py:12
  747.4 13.3 %collective-permute-start.1 = (bf16[2,128,128]{2,1,0:T(8,128)(2,1)S(1)}, bf16[2,128,128]{2,1,0:T(8,128)(2,1)S(1)}, u32[]{:S(2)}, u32[]{:S(2)}) collective-permute-start(bf16[2,128,128]{2,1,0:T(8,128)(2,1)S(1)} %get-tuple-element.318), channel_id=1, source_target_pairs={{0,8},{8,16},{16,24},{24,32},{32,40},{40,48},{48,56},{56,64},{64,7... | collective-permute-start | bytes 196616 | tf_op jit(solution)/shard_map/while/body/eval_jaxpr/ppermute | solution.py:12
  761.3 13.3 %collective-permute-start.1 = (bf16[2,128,128]{2,1,0:T(8,128)(2,1)S(1)}, bf16[2,128,128]{2,1,0:T(8,128)(2,1)S(1)}, u32[]{:S(2)}, u32[]{:S(2)}) collective-permute-start(bf16[2,128,128]{2,1,0:T(8,128)(2,1)S(1)} %get-tuple-element.318), channel_id=1, source_target_pairs={{0,8},{8,16},{16,24},{24,32},{32,40},{40,48},{48,56},{56,64},{64,7... | collective-permute-start | bytes 196616 | tf_op jit(solution)/shard_map/while/body/eval_jaxpr/ppermute | solution.py:12
  775.3 13.3 %collective-permute-start.1 = (bf16[2,128,128]{2,1,0:T(8,128)(2,1)S(1)}, bf16[2,128,128]{2,1,0:T(8,128)(2,1)S(1)}, u32[]{:S(2)}, u32[]{:S(2)}) collective-permute-start(bf16[2,128,128]{2,1,0:T(8,128)(2,1)S(1)} %get-tuple-element.318), channel_id=1, source_target_pairs={{0,8},{8,16},{16,24},{24,32},{32,40},{40,48},{48,56},{56,64},{64,7... | collective-permute-start | bytes 196616 | tf_op jit(solution)/shard_map/while/body/eval_jaxpr/ppermute | solution.py:12
  789.2 13.3 %collective-permute-start.1 = (bf16[2,128,128]{2,1,0:T(8,128)(2,1)S(1)}, bf16[2,128,128]{2,1,0:T(8,128)(2,1)S(1)}, u32[]{:S(2)}, u32[]{:S(2)}) collective-permute-start(bf16[2,128,128]{2,1,0:T(8,128)(2,1)S(1)} %get-tuple-element.318), channel_id=1, source_target_pairs={{0,8},{8,16},{16,24},{24,32},{32,40},{40,48},{48,56},{56,64},{64,7... | collective-permute-start | bytes 196616 | tf_op jit(solution)/shard_map/while/body/eval_jaxpr/ppermute | solution.py:12
  803.1 13.3 %collective-permute-start.1 = (bf16[2,128,128]{2,1,0:T(8,128)(2,1)S(1)}, bf16[2,128,128]{2,1,0:T(8,128)(2,1)S(1)}, u32[]{:S(2)}, u32[]{:S(2)}) collective-permute-start(bf16[2,128,128]{2,1,0:T(8,128)(2,1)S(1)} %get-tuple-element.318), channel_id=1, source_target_pairs={{0,8},{8,16},{16,24},{24,32},{32,40},{40,48},{48,56},{56,64},{64,7... | collective-permute-start | bytes 196616 | tf_op jit(solution)/shard_map/while/body/eval_jaxpr/ppermute | solution.py:12
  817.0 13.3 %collective-permute-start.1 = (bf16[2,128,128]{2,1,0:T(8,128)(2,1)S(1)}, bf16[2,128,128]{2,1,0:T(8,128)(2,1)S(1)}, u32[]{:S(2)}, u32[]{:S(2)}) collective-permute-start(bf16[2,128,128]{2,1,0:T(8,128)(2,1)S(1)} %get-tuple-element.318), channel_id=1, source_target_pairs={{0,8},{8,16},{16,24},{24,32},{32,40},{40,48},{48,56},{56,64},{64,7... | collective-permute-start | bytes 196616 | tf_op jit(solution)/shard_map/while/body/eval_jaxpr/ppermute | solution.py:12
  830.9 13.3 %collective-permute-start.1 = (bf16[2,128,128]{2,1,0:T(8,128)(2,1)S(1)}, bf16[2,128,128]{2,1,0:T(8,128)(2,1)S(1)}, u32[]{:S(2)}, u32[]{:S(2)}) collective-permute-start(bf16[2,128,128]{2,1,0:T(8,128)(2,1)S(1)} %get-tuple-element.318), channel_id=1, source_target_pairs={{0,8},{8,16},{16,24},{24,32},{32,40},{40,48},{48,56},{56,64},{64,7... | collective-permute-start | bytes 196616 | tf_op jit(solution)/shard_map/while/body/eval_jaxpr/ppermute | solution.py:12
  844.9 13.3 %collective-permute-start.1 = (bf16[2,128,128]{2,1,0:T(8,128)(2,1)S(1)}, bf16[2,128,128]{2,1,0:T(8,128)(2,1)S(1)}, u32[]{:S(2)}, u32[]{:S(2)}) collective-permute-start(bf16[2,128,128]{2,1,0:T(8,128)(2,1)S(1)} %get-tuple-element.318), channel_id=1, source_target_pairs={{0,8},{8,16},{16,24},{24,32},{32,40},{40,48},{48,56},{56,64},{64,7... | collective-permute-start | bytes 196616 | tf_op jit(solution)/shard_map/while/body/eval_jaxpr/ppermute | solution.py:12
  858.8 13.3 %collective-permute-start.1 = (bf16[2,128,128]{2,1,0:T(8,128)(2,1)S(1)}, bf16[2,128,128]{2,1,0:T(8,128)(2,1)S(1)}, u32[]{:S(2)}, u32[]{:S(2)}) collective-permute-start(bf16[2,128,128]{2,1,0:T(8,128)(2,1)S(1)} %get-tuple-element.318), channel_id=1, source_target_pairs={{0,8},{8,16},{16,24},{24,32},{32,40},{40,48},{48,56},{56,64},{64,7... | collective-permute-start | bytes 196616 | tf_op jit(solution)/shard_map/while/body/eval_jaxpr/ppermute | solution.py:12
  872.7 13.3 %collective-permute-start.1 = (bf16[2,128,128]{2,1,0:T(8,128)(2,1)S(1)}, bf16[2,128,128]{2,1,0:T(8,128)(2,1)S(1)}, u32[]{:S(2)}, u32[]{:S(2)}) collective-permute-start(bf16[2,128,128]{2,1,0:T(8,128)(2,1)S(1)} %get-tuple-element.318), channel_id=1, source_target_pairs={{0,8},{8,16},{16,24},{24,32},{32,40},{40,48},{48,56},{56,64},{64,7... | collective-permute-start | bytes 196616 | tf_op jit(solution)/shard_map/while/body/eval_jaxpr/ppermute | solution.py:12
  886.6 13.3 %collective-permute-start.1 = (bf16[2,128,128]{2,1,0:T(8,128)(2,1)S(1)}, bf16[2,128,128]{2,1,0:T(8,128)(2,1)S(1)}, u32[]{:S(2)}, u32[]{:S(2)}) collective-permute-start(bf16[2,128,128]{2,1,0:T(8,128)(2,1)S(1)} %get-tuple-element.318), channel_id=1, source_target_pairs={{0,8},{8,16},{16,24},{24,32},{32,40},{40,48},{48,56},{56,64},{64,7... | collective-permute-start | bytes 196616 | tf_op jit(solution)/shard_map/while/body/eval_jaxpr/ppermute | solution.py:12
  900.6 13.3 %collective-permute-start.1 = (bf16[2,128,128]{2,1,0:T(8,128)(2,1)S(1)}, bf16[2,128,128]{2,1,0:T(8,128)(2,1)S(1)}, u32[]{:S(2)}, u32[]{:S(2)}) collective-permute-start(bf16[2,128,128]{2,1,0:T(8,128)(2,1)S(1)} %get-tuple-element.318), channel_id=1, source_target_pairs={{0,8},{8,16},{16,24},{24,32},{32,40},{40,48},{48,56},{56,64},{64,7... | collective-permute-start | bytes 196616 | tf_op jit(solution)/shard_map/while/body/eval_jaxpr/ppermute | solution.py:12
  914.5 13.3 %collective-permute-start.1 = (bf16[2,128,128]{2,1,0:T(8,128)(2,1)S(1)}, bf16[2,128,128]{2,1,0:T(8,128)(2,1)S(1)}, u32[]{:S(2)}, u32[]{:S(2)}) collective-permute-start(bf16[2,128,128]{2,1,0:T(8,128)(2,1)S(1)} %get-tuple-element.318), channel_id=1, source_target_pairs={{0,8},{8,16},{16,24},{24,32},{32,40},{40,48},{48,56},{56,64},{64,7... | collective-permute-start | bytes 196616 | tf_op jit(solution)/shard_map/while/body/eval_jaxpr/ppermute | solution.py:12
  928.4 13.3 %collective-permute-start.1 = (bf16[2,128,128]{2,1,0:T(8,128)(2,1)S(1)}, bf16[2,128,128]{2,1,0:T(8,128)(2,1)S(1)}, u32[]{:S(2)}, u32[]{:S(2)}) collective-permute-start(bf16[2,128,128]{2,1,0:T(8,128)(2,1)S(1)} %get-tuple-element.318), channel_id=1, source_target_pairs={{0,8},{8,16},{16,24},{24,32},{32,40},{40,48},{48,56},{56,64},{64,7... | collective-permute-start | bytes 196616 | tf_op jit(solution)/shard_map/while/body/eval_jaxpr/ppermute | solution.py:12
  942.3 13.3 %collective-permute-start.1 = (bf16[2,128,128]{2,1,0:T(8,128)(2,1)S(1)}, bf16[2,128,128]{2,1,0:T(8,128)(2,1)S(1)}, u32[]{:S(2)}, u32[]{:S(2)}) collective-permute-start(bf16[2,128,128]{2,1,0:T(8,128)(2,1)S(1)} %get-tuple-element.318), channel_id=1, source_target_pairs={{0,8},{8,16},{16,24},{24,32},{32,40},{40,48},{48,56},{56,64},{64,7... | collective-permute-start | bytes 196616 | tf_op jit(solution)/shard_map/while/body/eval_jaxpr/ppermute | solution.py:12
  956.3 13.3 %collective-permute-start.1 = (bf16[2,128,128]{2,1,0:T(8,128)(2,1)S(1)}, bf16[2,128,128]{2,1,0:T(8,128)(2,1)S(1)}, u32[]{:S(2)}, u32[]{:S(2)}) collective-permute-start(bf16[2,128,128]{2,1,0:T(8,128)(2,1)S(1)} %get-tuple-element.318), channel_id=1, source_target_pairs={{0,8},{8,16},{16,24},{24,32},{32,40},{40,48},{48,56},{56,64},{64,7... | collective-permute-start | bytes 196616 | tf_op jit(solution)/shard_map/while/body/eval_jaxpr/ppermute | solution.py:12
  970.2 13.3 %collective-permute-start.1 = (bf16[2,128,128]{2,1,0:T(8,128)(2,1)S(1)}, bf16[2,128,128]{2,1,0:T(8,128)(2,1)S(1)}, u32[]{:S(2)}, u32[]{:S(2)}) collective-permute-start(bf16[2,128,128]{2,1,0:T(8,128)(2,1)S(1)} %get-tuple-element.318), channel_id=1, source_target_pairs={{0,8},{8,16},{16,24},{24,32},{32,40},{40,48},{48,56},{56,64},{64,7... | collective-permute-start | bytes 196616 | tf_op jit(solution)/shard_map/while/body/eval_jaxpr/ppermute | solution.py:12
  984.1 13.3 %collective-permute-start.1 = (bf16[2,128,128]{2,1,0:T(8,128)(2,1)S(1)}, bf16[2,128,128]{2,1,0:T(8,128)(2,1)S(1)}, u32[]{:S(2)}, u32[]{:S(2)}) collective-permute-start(bf16[2,128,128]{2,1,0:T(8,128)(2,1)S(1)} %get-tuple-element.318), channel_id=1, source_target_pairs={{0,8},{8,16},{16,24},{24,32},{32,40},{40,48},{48,56},{56,64},{64,7... | collective-permute-start | bytes 196616 | tf_op jit(solution)/shard_map/while/body/eval_jaxpr/ppermute | solution.py:12
  998.0 13.3 %collective-permute-start.1 = (bf16[2,128,128]{2,1,0:T(8,128)(2,1)S(1)}, bf16[2,128,128]{2,1,0:T(8,128)(2,1)S(1)}, u32[]{:S(2)}, u32[]{:S(2)}) collective-permute-start(bf16[2,128,128]{2,1,0:T(8,128)(2,1)S(1)} %get-tuple-element.318), channel_id=1, source_target_pairs={{0,8},{8,16},{16,24},{24,32},{32,40},{40,48},{48,56},{56,64},{64,7... | collective-permute-start | bytes 196616 | tf_op jit(solution)/shard_map/while/body/eval_jaxpr/ppermute | solution.py:12
  1011.9 13.3 %collective-permute-start.1 = (bf16[2,128,128]{2,1,0:T(8,128)(2,1)S(1)}, bf16[2,128,128]{2,1,0:T(8,128)(2,1)S(1)}, u32[]{:S(2)}, u32[]{:S(2)}) collective-permute-start(bf16[2,128,128]{2,1,0:T(8,128)(2,1)S(1)} %get-tuple-element.318), channel_id=1, source_target_pairs={{0,8},{8,16},{16,24},{24,32},{32,40},{40,48},{48,56},{56,64},{64,7... | collective-permute-start | bytes 196616 | tf_op jit(solution)/shard_map/while/body/eval_jaxpr/ppermute | solution.py:12
  1025.9 13.3 %collective-permute-start.1 = (bf16[2,128,128]{2,1,0:T(8,128)(2,1)S(1)}, bf16[2,128,128]{2,1,0:T(8,128)(2,1)S(1)}, u32[]{:S(2)}, u32[]{:S(2)}) collective-permute-start(bf16[2,128,128]{2,1,0:T(8,128)(2,1)S(1)} %get-tuple-element.318), channel_id=1, source_target_pairs={{0,8},{8,16},{16,24},{24,32},{32,40},{40,48},{48,56},{56,64},{64,7... | collective-permute-start | bytes 196616 | tf_op jit(solution)/shard_map/while/body/eval_jaxpr/ppermute | solution.py:12
  (68 other events, 2319.0 us)
Sparse Core Ops, SparseCore 0:
  10.8 85.6 all-gather.2
  98.5 65.5 all-gather.4
where the time goes:
time: 1090 us; the launch traced here: 1080 us
  waiting for transfers between devices  494 us (45%)
  starting transfers between devices  302 us (28%)
  loops' own time  196 us (18%)
  other arithmetic  50.1 us (5%)
  local copies, waits for them, and re-layouts  16.1 us (1%)
  between operations  14.9 us (1%)
  matrix products  11.9 us (1%)
    ppermute x126, waiting for transfers between devices, passed_along(): lax.ppermute(value, axis, [(source, source + steps) for source in range(l...  340 us
    ppermute x126, starting transfers between devices, passed_along(): lax.ppermute(value, axis, [(source, source + steps) for source in range(l...  302 us
    another operation x1, loops' own time, per_device(): lax.fori_loop(0, lax.axis_size('ctx') - 1, hand_round, (own_pair, start_p...  194 us
    all_gather x1, waiting for transfers between devices, per_device(): lax.all_gather(w_qkv, 'ctx', axis=1, tiled=True)  84.4 us
    all_gather x1, waiting for transfers between devices, per_device(): whole = lax.all_gather(tokens, 'head', axis=1, tiled=True)  67.6 us
    add x63, other arithmetic, combine(): later_state + jnp.where(linked, first_state, 0.0)  40.5 us
  transfers between devices with their start and end apart: 128, of which 65 were waited for; matrix products, arithmetic and copies ran while one was open for 0% of the time, Pallas kernels for 0%

commit v1 on v0

--- a/solution.py
+++ b/solution.py
@@ -4,6 +4,12 @@
 from jax.sharding import PartitionSpec as P
 
 HEAD_DIM = 128
+
+
+def gather_by_exchange(x, axis, dim):
+    size = lax.axis_size(axis)
+    repeats = [size if d == dim else 1 for d in range(x.ndim)]
+    return lax.all_to_all(jnp.tile(x, repeats), axis, split_axis=dim, concat_axis=dim, tiled=True)
 
 
 def passed_along(value, axis, steps):
@@ -71,7 +77,7 @@
     projected = jnp.einsum(
         "tr,grc->gtc",
         whole,
-        lax.all_gather(w_qkv, "ctx", axis=1, tiled=True),
+        gather_by_exchange(w_qkv, "ctx", 1),
         preferred_element_type=jnp.float32,
     ).astype(jnp.bfloat16)
     queries, key_map, values, seg_float, kv_state, tail_id = prepare(projected, seg_ids)

time: 1090 us -> 1050 us (0.963)
  waiting for transfers between devices: 494 us -> 430 us
  local copies, waits for them, and re-layouts: 16.1 us -> 34.5 us
  loops' own time: 196 us -> 208 us
    all_to_all x0 -> x1, waiting for transfers between devices: none -> 88.8 us  [gather_by_exchange(): lax.all_to_all(jnp.tile(x, repeats), axis, split_axis=dim, concat_axis=di...]
    all_gather x1 -> x0, waiting for transfers between devices: 84.4 us -> none  [per_device(): lax.all_gather(w_qkv, 'ctx', axis=1, tiled=True)]
    all_gather x1, waiting for transfers between devices: 67.6 us -> 0.01 us  [per_device(): whole = lax.all_gather(tokens, 'head', axis=1, tiled=True)]
    another operation x0 -> x2, local copies, waits for them, and re-layouts: none -> 18.3 us  [gather_by_exchange(): jnp.tile(x, repeats)]
    another operation x1, loops' own time: 194 us -> 206 us  [per_device(): lax.fori_loop(0, lax.axis_size('ctx') - 1, hand_round, (own_pair, start_p...]
  transfers between devices with their start and end apart: 128 -> 128, of which waited for: 65 -> 64; matrix products, arithmetic and copies ran while one was open for 0% -> 2% of each run, Pallas kernels for 0% -> 0%
where the time goes in v1:
time: 1050 us
  waiting for transfers between devices  430 us (41%)
  starting transfers between devices  303 us (29%)
  loops' own time  208 us (20%)
  other arithmetic  43.2 us (4%)
  local copies, waits for them, and re-layouts  34.5 us (3%)
  between operations  15 us (1%)
  matrix products  12.4 us (1%)
    ppermute x126, waiting for transfers between devices, passed_along(): lax.ppermute(value, axis, [(source, source + steps) for source in range(l...  341 us
    ppermute x126, starting transfers between devices, passed_along(): lax.ppermute(value, axis, [(source, source + steps) for source in range(l...  292 us
    another operation x1, loops' own time, per_device(): lax.fori_loop(0, lax.axis_size('ctx') - 1, hand_round, (own_pair, start_p...  206 us
    all_to_all x1, waiting for transfers between devices, gather_by_exchange(): lax.all_to_all(jnp.tile(x, repeats), axis, split_axis=dim, concat_axis=di...  88.8 us
    add x63, other arithmetic, combine(): later_state + jnp.where(linked, first_state, 0.0)  40.5 us
  transfers between devices with their start and end apart: 128, of which 64 were waited for; matrix products, arithmetic and copies ran while one was open for 2% of the time, Pallas kernels for 0%

profile of v1, /device:TPU:32, one launch (start us, length us, event | category | flops | bytes accessed | tf_op | source)
XLA Modules:
  0.0 1045.7 jit_solution(8556572639734646609)
XLA Ops:
  8.4 17.2 %copy.33 = bf16[3,2048,256]{2,0,1:T(4,128)(2,1)} copy(bf16[3,2048,256]{2,1,0:T(8,128)(2,1)S(1)} %bitcast.42) | data formatting | bytes 6291456 | tf_op jit(solution)/shard_map/tile | solution.py:12
  25.6 10.9 %all-to-all-start = ((bf16[3,2048,256]{2,0,1:T(4,128)(2,1)}), bf16[3,2048,256]{2,0,1:T(4,128)(2,1)}, u32[]{:S(2)}, u32[]{:S(2)}) async-start(bf16[3,2048,256]{2,0,1:T(4,128)(2,1)} %copy.33), calls=%async_computation | async-start | bytes 8388608 | tf_op jit(solution)/shard_map/all_to_all | solution.py:12
  39.3 88.8 %all-to-all-done = bf16[3,2048,256]{2,0,1:T(4,128)(2,1)} async-done(((bf16[3,2048,256]{2,0,1:T(4,128)(2,1)}), bf16[3,2048,256]{2,0,1:T(4,128)(2,1)}, u32[]{:S(2)}, u32[]{:S(2)}) %all-to-all-start) | async-done | bytes 3145760 | tf_op jit(solution)/shard_map/all_to_all | solution.py:12
  128.0 6.9 fusion.18
  138.2 879.7 %while.28 = (s32[]{:T(128)}, bf16[2,128,128]{2,1,0:T(8,128)(2,1)S(1)}, bf16[]{:T(256)}, bf16[2,128,128]{2,1,0:T(8,128)(2,1)}, f32[]{:T(128)}, /*index=5*/f32[]{:...) while((s32[]{:T(128)}, bf16[2,128,128]{2,1,0:T(8,128)(2,1)S(1)}, bf16[]{:T(256)}, ...), condition=%wide.region_3.4_spmd, body=%wide.region_2.3_spmd.sunk | while | flops 163846 | bytes 590031 | solution.py:96
  156.9 5.4 collective-permute-done
  170.8 5.4 collective-permute-done
  184.8 5.4 collective-permute-done
  198.8 5.4 collective-permute-done
  212.7 5.4 collective-permute-done
  226.7 5.4 collective-permute-done
  240.7 5.4 collective-permute-done
  254.6 5.4 collective-permute-done
  268.6 5.4 collective-permute-done
  282.5 5.4 collective-permute-done
  296.5 5.4 collective-permute-done
  310.5 5.4 collective-permute-done
  324.4 5.4 collective-permute-done
  338.4 5.4 collective-permute-done
  352.3 5.4 collective-permute-done
  366.3 5.4 collective-permute-done
  380.3 5.4 collective-permute-done
  394.2 5.4 collective-permute-done
  408.2 5.4 collective-permute-done
  422.2 5.4 collective-permute-done
  436.1 5.4 collective-permute-done
  450.1 5.4 collective-permute-done
  464.0 5.4 collective-permute-done
  478.0 5.4 collective-permute-done
  492.0 5.4 collective-permute-done
  505.9 5.4 collective-permute-done
  519.9 5.4 collective-permute-done
  533.8 5.4 collective-permute-done
  547.8 5.4 collective-permute-done
  561.8 5.4 collective-permute-done
  575.7 5.4 collective-permute-done
  589.7 5.4 collective-permute-done
  603.7 5.4 collective-permute-done
  617.6 5.4 collective-permute-done
  631.6 5.4 collective-permute-done
  645.5 5.4 collective-permute-done
  659.5 5.4 collective-permute-done
  673.5 5.4 collective-permute-done
  687.4 5.4 collective-permute-done
  701.4 5.4 collective-permute-done
  715.3 5.4 collective-permute-done
  729.3 5.4 collective-permute-done
  743.3 5.4 collective-permute-done
  757.2 5.4 collective-permute-done
  771.2 5.4 collective-permute-done
  785.2 5.4 collective-permute-done
  799.1 5.4 collective-permute-done
  813.1 5.4 collective-permute-done
  827.0 5.4 collective-permute-done
  841.0 5.4 collective-permute-done
  855.0 5.4 collective-permute-done
  868.9 5.4 collective-permute-done
  882.9 5.4 collective-permute-done
  896.8 5.4 collective-permute-done
  910.8 5.4 collective-permute-done
  924.8 5.4 collective-permute-done
  938.7 5.4 collective-permute-done
  952.7 5.4 collective-permute-done
  1017.9 18.5 %while.29 = (s32[]{:T(128)}, f32[2,512,2,128]{1,0,3,2:T(2,128)S(1)}, s32[2]{0:T(128)S(1)}, f32[1024]{0:T(1024)S(1)}, bf16[1024,2,128]{2,0,1:T(8,128)(2,1)S(1)}, ...) while((s32[]{:T(128)}, ...), condition=%wide.region_1.2_spmd.clone, body=%wide.region_0.1_spmd.clone.sunk | while | flops 540541440 | bytes 4995255 | solution.py:68
  (305 shorter events, 385.9 us)
Async XLA Ops:
  6.5 121.5 %all-gather.2.cloned.1.call-start = ((), (), s32[]{:S(2)}) async-start(), calls=%async_computation.1 | async-start | bytes 4718592 | tf_op jit(solution)/shard_map/all_gather | solution.py:76
  25.6 102.4 %all-to-all-start = ((bf16[3,2048,256]{2,0,1:T(4,128)(2,1)}), bf16[3,2048,256]{2,0,1:T(4,128)(2,1)}, u32[]{:S(2)}, u32[]{:S(2)}) async-start(bf16[3,2048,256]{2,0,1:T(4,128)(2,1)} %copy.33), calls=%async_computation | async-start | bytes 8388608 | tf_op jit(solution)/shard_map/all_to_all | solution.py:12
  138.2 13.4 %collective-permute-start.1 = (bf16[2,128,128]{2,1,0:T(8,128)(2,1)S(1)}, bf16[2,128,128]{2,1,0:T(8,128)(2,1)S(1)}, u32[]{:S(2)}, u32[]{:S(2)}) collective-permute-start(bf16[2,128,128]{2,1,0:T(8,128)(2,1)S(1)} %get-tuple-element.332), channel_id=1, source_target_pairs={{0,8},{8,16},{16,24},{24,32},{32,40},{40,48},{48,56},{56,64},{64,7... | collective-permute-start | bytes 196616 | tf_op jit(solution)/shard_map/while/body/eval_jaxpr/ppermute | solution.py:18
  152.2 13.3 %collective-permute-start.1 = (bf16[2,128,128]{2,1,0:T(8,128)(2,1)S(1)}, bf16[2,128,128]{2,1,0:T(8,128)(2,1)S(1)}, u32[]{:S(2)}, u32[]{:S(2)}) collective-permute-start(bf16[2,128,128]{2,1,0:T(8,128)(2,1)S(1)} %get-tuple-element.332), channel_id=1, source_target_pairs={{0,8},{8,16},{16,24},{24,32},{32,40},{40,48},{48,56},{56,64},{64,7... | collective-permute-start | bytes 196616 | tf_op jit(solution)/shard_map/while/body/eval_jaxpr/ppermute | solution.py:18
  166.2 13.3 %collective-permute-start.1 = (bf16[2,128,128]{2,1,0:T(8,128)(2,1)S(1)}, bf16[2,128,128]{2,1,0:T(8,128)(2,1)S(1)}, u32[]{:S(2)}, u32[]{:S(2)}) collective-permute-start(bf16[2,128,128]{2,1,0:T(8,128)(2,1)S(1)} %get-tuple-element.332), channel_id=1, source_target_pairs={{0,8},{8,16},{16,24},{24,32},{32,40},{40,48},{48,56},{56,64},{64,7... | collective-permute-start | bytes 196616 | tf_op jit(solution)/shard_map/while/body/eval_jaxpr/ppermute | solution.py:18
  180.2 13.3 %collective-permute-start.1 = (bf16[2,128,128]{2,1,0:T(8,128)(2,1)S(1)}, bf16[2,128,128]{2,1,0:T(8,128)(2,1)S(1)}, u32[]{:S(2)}, u32[]{:S(2)}) collective-permute-start(bf16[2,128,128]{2,1,0:T(8,128)(2,1)S(1)} %get-tuple-element.332), channel_id=1, source_target_pairs={{0,8},{8,16},{16,24},{24,32},{32,40},{40,48},{48,56},{56,64},{64,7... | collective-permute-start | bytes 196616 | tf_op jit(solution)/shard_map/while/body/eval_jaxpr/ppermute | solution.py:18
  194.1 13.3 %collective-permute-start.1 = (bf16[2,128,128]{2,1,0:T(8,128)(2,1)S(1)}, bf16[2,128,128]{2,1,0:T(8,128)(2,1)S(1)}, u32[]{:S(2)}, u32[]{:S(2)}) collective-permute-start(bf16[2,128,128]{2,1,0:T(8,128)(2,1)S(1)} %get-tuple-element.332), channel_id=1, source_target_pairs={{0,8},{8,16},{16,24},{24,32},{32,40},{40,48},{48,56},{56,64},{64,7... | collective-permute-start | bytes 196616 | tf_op jit(solution)/shard_map/while/body/eval_jaxpr/ppermute | solution.py:18
  208.1 13.3 %collective-permute-start.1 = (bf16[2,128,128]{2,1,0:T(8,128)(2,1)S(1)}, bf16[2,128,128]{2,1,0:T(8,128)(2,1)S(1)}, u32[]{:S(2)}, u32[]{:S(2)}) collective-permute-start(bf16[2,128,128]{2,1,0:T(8,128)(2,1)S(1)} %get-tuple-element.332), channel_id=1, source_target_pairs={{0,8},{8,16},{16,24},{24,32},{32,40},{40,48},{48,56},{56,64},{64,7... | collective-permute-start | bytes 196616 | tf_op jit(solution)/shard_map/while/body/eval_jaxpr/ppermute | solution.py:18
  222.0 13.3 %collective-permute-start.1 = (bf16[2,128,128]{2,1,0:T(8,128)(2,1)S(1)}, bf16[2,128,128]{2,1,0:T(8,128)(2,1)S(1)}, u32[]{:S(2)}, u32[]{:S(2)}) collective-permute-start(bf16[2,128,128]{2,1,0:T(8,128)(2,1)S(1)} %get-tuple-element.332), channel_id=1, source_target_pairs={{0,8},{8,16},{16,24},{24,32},{32,40},{40,48},{48,56},{56,64},{64,7... | collective-permute-start | bytes 196616 | tf_op jit(solution)/shard_map/while/body/eval_jaxpr/ppermute | solution.py:18
  236.0 13.3 %collective-permute-start.1 = (bf16[2,128,128]{2,1,0:T(8,128)(2,1)S(1)}, bf16[2,128,128]{2,1,0:T(8,128)(2,1)S(1)}, u32[]{:S(2)}, u32[]{:S(2)}) collective-permute-start(bf16[2,128,128]{2,1,0:T(8,128)(2,1)S(1)} %get-tuple-element.332), channel_id=1, source_target_pairs={{0,8},{8,16},{16,24},{24,32},{32,40},{40,48},{48,56},{56,64},{64,7... | collective-permute-start | bytes 196616 | tf_op jit(solution)/shard_map/while/body/eval_jaxpr/ppermute | solution.py:18
  250.0 13.3 %collective-permute-start.1 = (bf16[2,128,128]{2,1,0:T(8,128)(2,1)S(1)}, bf16[2,128,128]{2,1,0:T(8,128)(2,1)S(1)}, u32[]{:S(2)}, u32[]{:S(2)}) collective-permute-start(bf16[2,128,128]{2,1,0:T(8,128)(2,1)S(1)} %get-tuple-element.332), channel_id=1, source_target_pairs={{0,8},{8,16},{16,24},{24,32},{32,40},{40,48},{48,56},{56,64},{64,7... | collective-permute-start | bytes 196616 | tf_op jit(solution)/shard_map/while/body/eval_jaxpr/ppermute | solution.py:18
  263.9 13.3 %collective-permute-start.1 = (bf16[2,128,128]{2,1,0:T(8,128)(2,1)S(1)}, bf16[2,128,128]{2,1,0:T(8,128)(2,1)S(1)}, u32[]{:S(2)}, u32[]{:S(2)}) collective-permute-start(bf16[2,128,128]{2,1,0:T(8,128)(2,1)S(1)} %get-tuple-element.332), channel_id=1, source_target_pairs={{0,8},{8,16},{16,24},{24,32},{32,40},{40,48},{48,56},{56,64},{64,7... | collective-permute-start | bytes 196616 | tf_op jit(solution)/shard_map/while/body/eval_jaxpr/ppermute | solution.py:18
  277.9 13.3 %collective-permute-start.1 = (bf16[2,128,128]{2,1,0:T(8,128)(2,1)S(1)}, bf16[2,128,128]{2,1,0:T(8,128)(2,1)S(1)}, u32[]{:S(2)}, u32[]{:S(2)}) collective-permute-start(bf16[2,128,128]{2,1,0:T(8,128)(2,1)S(1)} %get-tuple-element.332), channel_id=1, source_target_pairs={{0,8},{8,16},{16,24},{24,32},{32,40},{40,48},{48,56},{56,64},{64,7... | collective-permute-start | bytes 196616 | tf_op jit(solution)/shard_map/while/body/eval_jaxpr/ppermute | solution.py:18
  291.9 13.3 %collective-permute-start.1 = (bf16[2,128,128]{2,1,0:T(8,128)(2,1)S(1)}, bf16[2,128,128]{2,1,0:T(8,128)(2,1)S(1)}, u32[]{:S(2)}, u32[]{:S(2)}) collective-permute-start(bf16[2,128,128]{2,1,0:T(8,128)(2,1)S(1)} %get-tuple-element.332), channel_id=1, source_target_pairs={{0,8},{8,16},{16,24},{24,32},{32,40},{40,48},{48,56},{56,64},{64,7... | collective-permute-start | bytes 196616 | tf_op jit(solution)/shard_map/while/body/eval_jaxpr/ppermute | solution.py:18
  305.8 13.3 %collective-permute-start.1 = (bf16[2,128,128]{2,1,0:T(8,128)(2,1)S(1)}, bf16[2,128,128]{2,1,0:T(8,128)(2,1)S(1)}, u32[]{:S(2)}, u32[]{:S(2)}) collective-permute-start(bf16[2,128,128]{2,1,0:T(8,128)(2,1)S(1)} %get-tuple-element.332), channel_id=1, source_target_pairs={{0,8},{8,16},{16,24},{24,32},{32,40},{40,48},{48,56},{56,64},{64,7... | collective-permute-start | bytes 196616 | tf_op jit(solution)/shard_map/while/body/eval_jaxpr/ppermute | solution.py:18
  319.8 13.3 %collective-permute-start.1 = (bf16[2,128,128]{2,1,0:T(8,128)(2,1)S(1)}, bf16[2,128,128]{2,1,0:T(8,128)(2,1)S(1)}, u32[]{:S(2)}, u32[]{:S(2)}) collective-permute-start(bf16[2,128,128]{2,1,0:T(8,128)(2,1)S(1)} %get-tuple-element.332), channel_id=1, source_target_pairs={{0,8},{8,16},{16,24},{24,32},{32,40},{40,48},{48,56},{56,64},{64,7... | collective-permute-start | bytes 196616 | tf_op jit(solution)/shard_map/while/body/eval_jaxpr/ppermute | solution.py:18
  333.7 13.3 %collective-permute-start.1 = (bf16[2,128,128]{2,1,0:T(8,128)(2,1)S(1)}, bf16[2,128,128]{2,1,0:T(8,128)(2,1)S(1)}, u32[]{:S(2)}, u32[]{:S(2)}) collective-permute-start(bf16[2,128,128]{2,1,0:T(8,128)(2,1)S(1)} %get-tuple-element.332), channel_id=1, source_target_pairs={{0,8},{8,16},{16,24},{24,32},{32,40},{40,48},{48,56},{56,64},{64,7... | collective-permute-start | bytes 196616 | tf_op jit(solution)/shard_map/while/body/eval_jaxpr/ppermute | solution.py:18
  347.7 13.3 %collective-permute-start.1 = (bf16[2,128,128]{2,1,0:T(8,128)(2,1)S(1)}, bf16[2,128,128]{2,1,0:T(8,128)(2,1)S(1)}, u32[]{:S(2)}, u32[]{:S(2)}) collective-permute-start(bf16[2,128,128]{2,1,0:T(8,128)(2,1)S(1)} %get-tuple-element.332), channel_id=1, source_target_pairs={{0,8},{8,16},{16,24},{24,32},{32,40},{40,48},{48,56},{56,64},{64,7... | collective-permute-start | bytes 196616 | tf_op jit(solution)/shard_map/while/body/eval_jaxpr/ppermute | solution.py:18
  361.7 13.3 %collective-permute-start.1 = (bf16[2,128,128]{2,1,0:T(8,128)(2,1)S(1)}, bf16[2,128,128]{2,1,0:T(8,128)(2,1)S(1)}, u32[]{:S(2)}, u32[]{:S(2)}) collective-permute-start(bf16[2,128,128]{2,1,0:T(8,128)(2,1)S(1)} %get-tuple-element.332), channel_id=1, source_target_pairs={{0,8},{8,16},{16,24},{24,32},{32,40},{40,48},{48,56},{56,64},{64,7... | collective-permute-start | bytes 196616 | tf_op jit(solution)/shard_map/while/body/eval_jaxpr/ppermute | solution.py:18
  375.6 13.3 %collective-permute-start.1 = (bf16[2,128,128]{2,1,0:T(8,128)(2,1)S(1)}, bf16[2,128,128]{2,1,0:T(8,128)(2,1)S(1)}, u32[]{:S(2)}, u32[]{:S(2)}) collective-permute-start(bf16[2,128,128]{2,1,0:T(8,128)(2,1)S(1)} %get-tuple-element.332), channel_id=1, source_target_pairs={{0,8},{8,16},{16,24},{24,32},{32,40},{40,48},{48,56},{56,64},{64,7... | collective-permute-start | bytes 196616 | tf_op jit(solution)/shard_map/while/body/eval_jaxpr/ppermute | solution.py:18
  389.6 13.3 %collective-permute-start.1 = (bf16[2,128,128]{2,1,0:T(8,128)(2,1)S(1)}, bf16[2,128,128]{2,1,0:T(8,128)(2,1)S(1)}, u32[]{:S(2)}, u32[]{:S(2)}) collective-permute-start(bf16[2,128,128]{2,1,0:T(8,128)(2,1)S(1)} %get-tuple-element.332), channel_id=1, source_target_pairs={{0,8},{8,16},{16,24},{24,32},{32,40},{40,48},{48,56},{56,64},{64,7... | collective-permute-start | bytes 196616 | tf_op jit(solution)/shard_map/while/body/eval_jaxpr/ppermute | solution.py:18
  403.5 13.3 %collective-permute-start.1 = (bf16[2,128,128]{2,1,0:T(8,128)(2,1)S(1)}, bf16[2,128,128]{2,1,0:T(8,128)(2,1)S(1)}, u32[]{:S(2)}, u32[]{:S(2)}) collective-permute-start(bf16[2,128,128]{2,1,0:T(8,128)(2,1)S(1)} %get-tuple-element.332), channel_id=1, source_target_pairs={{0,8},{8,16},{16,24},{24,32},{32,40},{40,48},{48,56},{56,64},{64,7... | collective-permute-start | bytes 196616 | tf_op jit(solution)/shard_map/while/body/eval_jaxpr/ppermute | solution.py:18
  417.5 13.3 %collective-permute-start.1 = (bf16[2,128,128]{2,1,0:T(8,128)(2,1)S(1)}, bf16[2,128,128]{2,1,0:T(8,128)(2,1)S(1)}, u32[]{:S(2)}, u32[]{:S(2)}) collective-permute-start(bf16[2,128,128]{2,1,0:T(8,128)(2,1)S(1)} %get-tuple-element.332), channel_id=1, source_target_pairs={{0,8},{8,16},{16,24},{24,32},{32,40},{40,48},{48,56},{56,64},{64,7... | collective-permute-start | bytes 196616 | tf_op jit(solution)/shard_map/while/body/eval_jaxpr/ppermute | solution.py:18
  431.5 13.3 %collective-permute-start.1 = (bf16[2,128,128]{2,1,0:T(8,128)(2,1)S(1)}, bf16[2,128,128]{2,1,0:T(8,128)(2,1)S(1)}, u32[]{:S(2)}, u32[]{:S(2)}) collective-permute-start(bf16[2,128,128]{2,1,0:T(8,128)(2,1)S(1)} %get-tuple-element.332), channel_id=1, source_target_pairs={{0,8},{8,16},{16,24},{24,32},{32,40},{40,48},{48,56},{56,64},{64,7... | collective-permute-start | bytes 196616 | tf_op jit(solution)/shard_map/while/body/eval_jaxpr/ppermute | solution.py:18
  445.4 13.3 %collective-permute-start.1 = (bf16[2,128,128]{2,1,0:T(8,128)(2,1)S(1)}, bf16[2,128,128]{2,1,0:T(8,128)(2,1)S(1)}, u32[]{:S(2)}, u32[]{:S(2)}) collective-permute-start(bf16[2,128,128]{2,1,0:T(8,128)(2,1)S(1)} %get-tuple-element.332), channel_id=1, source_target_pairs={{0,8},{8,16},{16,24},{24,32},{32,40},{40,48},{48,56},{56,64},{64,7... | collective-permute-start | bytes 196616 | tf_op jit(solution)/shard_map/while/body/eval_jaxpr/ppermute | solution.py:18
  459.4 13.3 %collective-permute-start.1 = (bf16[2,128,128]{2,1,0:T(8,128)(2,1)S(1)}, bf16[2,128,128]{2,1,0:T(8,128)(2,1)S(1)}, u32[]{:S(2)}, u32[]{:S(2)}) collective-permute-start(bf16[2,128,128]{2,1,0:T(8,128)(2,1)S(1)} %get-tuple-element.332), channel_id=1, source_target_pairs={{0,8},{8,16},{16,24},{24,32},{32,40},{40,48},{48,56},{56,64},{64,7... | collective-permute-start | bytes 196616 | tf_op jit(solution)/shard_map/while/body/eval_jaxpr/ppermute | solution.py:18
  473.4 13.3 %collective-permute-start.1 = (bf16[2,128,128]{2,1,0:T(8,128)(2,1)S(1)}, bf16[2,128,128]{2,1,0:T(8,128)(2,1)S(1)}, u32[]{:S(2)}, u32[]{:S(2)}) collective-permute-start(bf16[2,128,128]{2,1,0:T(8,128)(2,1)S(1)} %get-tuple-element.332), channel_id=1, source_target_pairs={{0,8},{8,16},{16,24},{24,32},{32,40},{40,48},{48,56},{56,64},{64,7... | collective-permute-start | bytes 196616 | tf_op jit(solution)/shard_map/while/body/eval_jaxpr/ppermute | solution.py:18
  487.3 13.3 %collective-permute-start.1 = (bf16[2,128,128]{2,1,0:T(8,128)(2,1)S(1)}, bf16[2,128,128]{2,1,0:T(8,128)(2,1)S(1)}, u32[]{:S(2)}, u32[]{:S(2)}) collective-permute-start(bf16[2,128,128]{2,1,0:T(8,128)(2,1)S(1)} %get-tuple-element.332), channel_id=1, source_target_pairs={{0,8},{8,16},{16,24},{24,32},{32,40},{40,48},{48,56},{56,64},{64,7... | collective-permute-start | bytes 196616 | tf_op jit(solution)/shard_map/while/body/eval_jaxpr/ppermute | solution.py:18
  501.3 13.3 %collective-permute-start.1 = (bf16[2,128,128]{2,1,0:T(8,128)(2,1)S(1)}, bf16[2,128,128]{2,1,0:T(8,128)(2,1)S(1)}, u32[]{:S(2)}, u32[]{:S(2)}) collective-permute-start(bf16[2,128,128]{2,1,0:T(8,128)(2,1)S(1)} %get-tuple-element.332), channel_id=1, source_target_pairs={{0,8},{8,16},{16,24},{24,32},{32,40},{40,48},{48,56},{56,64},{64,7... | collective-permute-start | bytes 196616 | tf_op jit(solution)/shard_map/while/body/eval_jaxpr/ppermute | solution.py:18
  515.2 13.3 %collective-permute-start.1 = (bf16[2,128,128]{2,1,0:T(8,128)(2,1)S(1)}, bf16[2,128,128]{2,1,0:T(8,128)(2,1)S(1)}, u32[]{:S(2)}, u32[]{:S(2)}) collective-permute-start(bf16[2,128,128]{2,1,0:T(8,128)(2,1)S(1)} %get-tuple-element.332), channel_id=1, source_target_pairs={{0,8},{8,16},{16,24},{24,32},{32,40},{40,48},{48,56},{56,64},{64,7... | collective-permute-start | bytes 196616 | tf_op jit(solution)/shard_map/while/body/eval_jaxpr/ppermute | solution.py:18
  529.2 13.3 %collective-permute-start.1 = (bf16[2,128,128]{2,1,0:T(8,128)(2,1)S(1)}, bf16[2,128,128]{2,1,0:T(8,128)(2,1)S(1)}, u32[]{:S(2)}, u32[]{:S(2)}) collective-permute-start(bf16[2,128,128]{2,1,0:T(8,128)(2,1)S(1)} %get-tuple-element.332), channel_id=1, source_target_pairs={{0,8},{8,16},{16,24},{24,32},{32,40},{40,48},{48,56},{56,64},{64,7... | collective-permute-start | bytes 196616 | tf_op jit(solution)/shard_map/while/body/eval_jaxpr/ppermute | solution.py:18
  543.2 13.3 %collective-permute-start.1 = (bf16[2,128,128]{2,1,0:T(8,128)(2,1)S(1)}, bf16[2,128,128]{2,1,0:T(8,128)(2,1)S(1)}, u32[]{:S(2)}, u32[]{:S(2)}) collective-permute-start(bf16[2,128,128]{2,1,0:T(8,128)(2,1)S(1)} %get-tuple-element.332), channel_id=1, source_target_pairs={{0,8},{8,16},{16,24},{24,32},{32,40},{40,48},{48,56},{56,64},{64,7... | collective-permute-start | bytes 196616 | tf_op jit(solution)/shard_map/while/body/eval_jaxpr/ppermute | solution.py:18
  557.1 13.3 %collective-permute-start.1 = (bf16[2,128,128]{2,1,0:T(8,128)(2,1)S(1)}, bf16[2,128,128]{2,1,0:T(8,128)(2,1)S(1)}, u32[]{:S(2)}, u32[]{:S(2)}) collective-permute-start(bf16[2,128,128]{2,1,0:T(8,128)(2,1)S(1)} %get-tuple-element.332), channel_id=1, source_target_pairs={{0,8},{8,16},{16,24},{24,32},{32,40},{40,48},{48,56},{56,64},{64,7... | collective-permute-start | bytes 196616 | tf_op jit(solution)/shard_map/while/body/eval_jaxpr/ppermute | solution.py:18
  571.1 13.3 %collective-permute-start.1 = (bf16[2,128,128]{2,1,0:T(8,128)(2,1)S(1)}, bf16[2,128,128]{2,1,0:T(8,128)(2,1)S(1)}, u32[]{:S(2)}, u32[]{:S(2)}) collective-permute-start(bf16[2,128,128]{2,1,0:T(8,128)(2,1)S(1)} %get-tuple-element.332), channel_id=1, source_target_pairs={{0,8},{8,16},{16,24},{24,32},{32,40},{40,48},{48,56},{56,64},{64,7... | collective-permute-start | bytes 196616 | tf_op jit(solution)/shard_map/while/body/eval_jaxpr/ppermute | solution.py:18
  585.0 13.3 %collective-permute-start.1 = (bf16[2,128,128]{2,1,0:T(8,128)(2,1)S(1)}, bf16[2,128,128]{2,1,0:T(8,128)(2,1)S(1)}, u32[]{:S(2)}, u32[]{:S(2)}) collective-permute-start(bf16[2,128,128]{2,1,0:T(8,128)(2,1)S(1)} %get-tuple-element.332), channel_id=1, source_target_pairs={{0,8},{8,16},{16,24},{24,32},{32,40},{40,48},{48,56},{56,64},{64,7... | collective-permute-start | bytes 196616 | tf_op jit(solution)/shard_map/while/body/eval_jaxpr/ppermute | solution.py:18
  599.0 13.3 %collective-permute-start.1 = (bf16[2,128,128]{2,1,0:T(8,128)(2,1)S(1)}, bf16[2,128,128]{2,1,0:T(8,128)(2,1)S(1)}, u32[]{:S(2)}, u32[]{:S(2)}) collective-permute-start(bf16[2,128,128]{2,1,0:T(8,128)(2,1)S(1)} %get-tuple-element.332), channel_id=1, source_target_pairs={{0,8},{8,16},{16,24},{24,32},{32,40},{40,48},{48,56},{56,64},{64,7... | collective-permute-start | bytes 196616 | tf_op jit(solution)/shard_map/while/body/eval_jaxpr/ppermute | solution.py:18
  613.0 13.3 %collective-permute-start.1 = (bf16[2,128,128]{2,1,0:T(8,128)(2,1)S(1)}, bf16[2,128,128]{2,1,0:T(8,128)(2,1)S(1)}, u32[]{:S(2)}, u32[]{:S(2)}) collective-permute-start(bf16[2,128,128]{2,1,0:T(8,128)(2,1)S(1)} %get-tuple-element.332), channel_id=1, source_target_pairs={{0,8},{8,16},{16,24},{24,32},{32,40},{40,48},{48,56},{56,64},{64,7... | collective-permute-start | bytes 196616 | tf_op jit(solution)/shard_map/while/body/eval_jaxpr/ppermute | solution.py:18
  626.9 13.3 %collective-permute-start.1 = (bf16[2,128,128]{2,1,0:T(8,128)(2,1)S(1)}, bf16[2,128,128]{2,1,0:T(8,128)(2,1)S(1)}, u32[]{:S(2)}, u32[]{:S(2)}) collective-permute-start(bf16[2,128,128]{2,1,0:T(8,128)(2,1)S(1)} %get-tuple-element.332), channel_id=1, source_target_pairs={{0,8},{8,16},{16,24},{24,32},{32,40},{40,48},{48,56},{56,64},{64,7... | collective-permute-start | bytes 196616 | tf_op jit(solution)/shard_map/while/body/eval_jaxpr/ppermute | solution.py:18
  640.9 13.3 %collective-permute-start.1 = (bf16[2,128,128]{2,1,0:T(8,128)(2,1)S(1)}, bf16[2,128,128]{2,1,0:T(8,128)(2,1)S(1)}, u32[]{:S(2)}, u32[]{:S(2)}) collective-permute-start(bf16[2,128,128]{2,1,0:T(8,128)(2,1)S(1)} %get-tuple-element.332), channel_id=1, source_target_pairs={{0,8},{8,16},{16,24},{24,32},{32,40},{40,48},{48,56},{56,64},{64,7... | collective-permute-start | bytes 196616 | tf_op jit(solution)/shard_map/while/body/eval_jaxpr/ppermute | solution.py:18
  654.9 13.3 %collective-permute-start.1 = (bf16[2,128,128]{2,1,0:T(8,128)(2,1)S(1)}, bf16[2,128,128]{2,1,0:T(8,128)(2,1)S(1)}, u32[]{:S(2)}, u32[]{:S(2)}) collective-permute-start(bf16[2,128,128]{2,1,0:T(8,128)(2,1)S(1)} %get-tuple-element.332), channel_id=1, source_target_pairs={{0,8},{8,16},{16,24},{24,32},{32,40},{40,48},{48,56},{56,64},{64,7... | collective-permute-start | bytes 196616 | tf_op jit(solution)/shard_map/while/body/eval_jaxpr/ppermute | solution.py:18
  668.8 13.3 %collective-permute-start.1 = (bf16[2,128,128]{2,1,0:T(8,128)(2,1)S(1)}, bf16[2,128,128]{2,1,0:T(8,128)(2,1)S(1)}, u32[]{:S(2)}, u32[]{:S(2)}) collective-permute-start(bf16[2,128,128]{2,1,0:T(8,128)(2,1)S(1)} %get-tuple-element.332), channel_id=1, source_target_pairs={{0,8},{8,16},{16,24},{24,32},{32,40},{40,48},{48,56},{56,64},{64,7... | collective-permute-start | bytes 196616 | tf_op jit(solution)/shard_map/while/body/eval_jaxpr/ppermute | solution.py:18
  682.8 13.3 %collective-permute-start.1 = (bf16[2,128,128]{2,1,0:T(8,128)(2,1)S(1)}, bf16[2,128,128]{2,1,0:T(8,128)(2,1)S(1)}, u32[]{:S(2)}, u32[]{:S(2)}) collective-permute-start(bf16[2,128,128]{2,1,0:T(8,128)(2,1)S(1)} %get-tuple-element.332), channel_id=1, source_target_pairs={{0,8},{8,16},{16,24},{24,32},{32,40},{40,48},{48,56},{56,64},{64,7... | collective-permute-start | bytes 196616 | tf_op jit(solution)/shard_map/while/body/eval_jaxpr/ppermute | solution.py:18
  696.7 13.3 %collective-permute-start.1 = (bf16[2,128,128]{2,1,0:T(8,128)(2,1)S(1)}, bf16[2,128,128]{2,1,0:T(8,128)(2,1)S(1)}, u32[]{:S(2)}, u32[]{:S(2)}) collective-permute-start(bf16[2,128,128]{2,1,0:T(8,128)(2,1)S(1)} %get-tuple-element.332), channel_id=1, source_target_pairs={{0,8},{8,16},{16,24},{24,32},{32,40},{40,48},{48,56},{56,64},{64,7... | collective-permute-start | bytes 196616 | tf_op jit(solution)/shard_map/while/body/eval_jaxpr/ppermute | solution.py:18
  710.7 13.3 %collective-permute-start.1 = (bf16[2,128,128]{2,1,0:T(8,128)(2,1)S(1)}, bf16[2,128,128]{2,1,0:T(8,128)(2,1)S(1)}, u32[]{:S(2)}, u32[]{:S(2)}) collective-permute-start(bf16[2,128,128]{2,1,0:T(8,128)(2,1)S(1)} %get-tuple-element.332), channel_id=1, source_target_pairs={{0,8},{8,16},{16,24},{24,32},{32,40},{40,48},{48,56},{56,64},{64,7... | collective-permute-start | bytes 196616 | tf_op jit(solution)/shard_map/while/body/eval_jaxpr/ppermute | solution.py:18
  724.7 13.3 %collective-permute-start.1 = (bf16[2,128,128]{2,1,0:T(8,128)(2,1)S(1)}, bf16[2,128,128]{2,1,0:T(8,128)(2,1)S(1)}, u32[]{:S(2)}, u32[]{:S(2)}) collective-permute-start(bf16[2,128,128]{2,1,0:T(8,128)(2,1)S(1)} %get-tuple-element.332), channel_id=1, source_target_pairs={{0,8},{8,16},{16,24},{24,32},{32,40},{40,48},{48,56},{56,64},{64,7... | collective-permute-start | bytes 196616 | tf_op jit(solution)/shard_map/while/body/eval_jaxpr/ppermute | solution.py:18
  738.6 13.3 %collective-permute-start.1 = (bf16[2,128,128]{2,1,0:T(8,128)(2,1)S(1)}, bf16[2,128,128]{2,1,0:T(8,128)(2,1)S(1)}, u32[]{:S(2)}, u32[]{:S(2)}) collective-permute-start(bf16[2,128,128]{2,1,0:T(8,128)(2,1)S(1)} %get-tuple-element.332), channel_id=1, source_target_pairs={{0,8},{8,16},{16,24},{24,32},{32,40},{40,48},{48,56},{56,64},{64,7... | collective-permute-start | bytes 196616 | tf_op jit(solution)/shard_map/while/body/eval_jaxpr/ppermute | solution.py:18
  752.6 13.3 %collective-permute-start.1 = (bf16[2,128,128]{2,1,0:T(8,128)(2,1)S(1)}, bf16[2,128,128]{2,1,0:T(8,128)(2,1)S(1)}, u32[]{:S(2)}, u32[]{:S(2)}) collective-permute-start(bf16[2,128,128]{2,1,0:T(8,128)(2,1)S(1)} %get-tuple-element.332), channel_id=1, source_target_pairs={{0,8},{8,16},{16,24},{24,32},{32,40},{40,48},{48,56},{56,64},{64,7... | collective-permute-start | bytes 196616 | tf_op jit(solution)/shard_map/while/body/eval_jaxpr/ppermute | solution.py:18
  766.5 13.3 %collective-permute-start.1 = (bf16[2,128,128]{2,1,0:T(8,128)(2,1)S(1)}, bf16[2,128,128]{2,1,0:T(8,128)(2,1)S(1)}, u32[]{:S(2)}, u32[]{:S(2)}) collective-permute-start(bf16[2,128,128]{2,1,0:T(8,128)(2,1)S(1)} %get-tuple-element.332), channel_id=1, source_target_pairs={{0,8},{8,16},{16,24},{24,32},{32,40},{40,48},{48,56},{56,64},{64,7... | collective-permute-start | bytes 196616 | tf_op jit(solution)/shard_map/while/body/eval_jaxpr/ppermute | solution.py:18
  780.5 13.3 %collective-permute-start.1 = (bf16[2,128,128]{2,1,0:T(8,128)(2,1)S(1)}, bf16[2,128,128]{2,1,0:T(8,128)(2,1)S(1)}, u32[]{:S(2)}, u32[]{:S(2)}) collective-permute-start(bf16[2,128,128]{2,1,0:T(8,128)(2,1)S(1)} %get-tuple-element.332), channel_id=1, source_target_pairs={{0,8},{8,16},{16,24},{24,32},{32,40},{40,48},{48,56},{56,64},{64,7... | collective-permute-start | bytes 196616 | tf_op jit(solution)/shard_map/while/body/eval_jaxpr/ppermute | solution.py:18
  794.5 13.3 %collective-permute-start.1 = (bf16[2,128,128]{2,1,0:T(8,128)(2,1)S(1)}, bf16[2,128,128]{2,1,0:T(8,128)(2,1)S(1)}, u32[]{:S(2)}, u32[]{:S(2)}) collective-permute-start(bf16[2,128,128]{2,1,0:T(8,128)(2,1)S(1)} %get-tuple-element.332), channel_id=1, source_target_pairs={{0,8},{8,16},{16,24},{24,32},{32,40},{40,48},{48,56},{56,64},{64,7... | collective-permute-start | bytes 196616 | tf_op jit(solution)/shard_map/while/body/eval_jaxpr/ppermute | solution.py:18
  808.4 13.3 %collective-permute-start.1 = (bf16[2,128,128]{2,1,0:T(8,128)(2,1)S(1)}, bf16[2,128,128]{2,1,0:T(8,128)(2,1)S(1)}, u32[]{:S(2)}, u32[]{:S(2)}) collective-permute-start(bf16[2,128,128]{2,1,0:T(8,128)(2,1)S(1)} %get-tuple-element.332), channel_id=1, source_target_pairs={{0,8},{8,16},{16,24},{24,32},{32,40},{40,48},{48,56},{56,64},{64,7... | collective-permute-start | bytes 196616 | tf_op jit(solution)/shard_map/while/body/eval_jaxpr/ppermute | solution.py:18
  822.4 13.3 %collective-permute-start.1 = (bf16[2,128,128]{2,1,0:T(8,128)(2,1)S(1)}, bf16[2,128,128]{2,1,0:T(8,128)(2,1)S(1)}, u32[]{:S(2)}, u32[]{:S(2)}) collective-permute-start(bf16[2,128,128]{2,1,0:T(8,128)(2,1)S(1)} %get-tuple-element.332), channel_id=1, source_target_pairs={{0,8},{8,16},{16,24},{24,32},{32,40},{40,48},{48,56},{56,64},{64,7... | collective-permute-start | bytes 196616 | tf_op jit(solution)/shard_map/while/body/eval_jaxpr/ppermute | solution.py:18
  836.4 13.3 %collective-permute-start.1 = (bf16[2,128,128]{2,1,0:T(8,128)(2,1)S(1)}, bf16[2,128,128]{2,1,0:T(8,128)(2,1)S(1)}, u32[]{:S(2)}, u32[]{:S(2)}) collective-permute-start(bf16[2,128,128]{2,1,0:T(8,128)(2,1)S(1)} %get-tuple-element.332), channel_id=1, source_target_pairs={{0,8},{8,16},{16,24},{24,32},{32,40},{40,48},{48,56},{56,64},{64,7... | collective-permute-start | bytes 196616 | tf_op jit(solution)/shard_map/while/body/eval_jaxpr/ppermute | solution.py:18
  864.3 13.3 %collective-permute-start.1 = (bf16[2,128,128]{2,1,0:T(8,128)(2,1)S(1)}, bf16[2,128,128]{2,1,0:T(8,128)(2,1)S(1)}, u32[]{:S(2)}, u32[]{:S(2)}) collective-permute-start(bf16[2,128,128]{2,1,0:T(8,128)(2,1)S(1)} %get-tuple-element.332), channel_id=1, source_target_pairs={{0,8},{8,16},{16,24},{24,32},{32,40},{40,48},{48,56},{56,64},{64,7... | collective-permute-start | bytes 196616 | tf_op jit(solution)/shard_map/while/body/eval_jaxpr/ppermute | solution.py:18
  878.2 13.3 %collective-permute-start.1 = (bf16[2,128,128]{2,1,0:T(8,128)(2,1)S(1)}, bf16[2,128,128]{2,1,0:T(8,128)(2,1)S(1)}, u32[]{:S(2)}, u32[]{:S(2)}) collective-permute-start(bf16[2,128,128]{2,1,0:T(8,128)(2,1)S(1)} %get-tuple-element.332), channel_id=1, source_target_pairs={{0,8},{8,16},{16,24},{24,32},{32,40},{40,48},{48,56},{56,64},{64,7... | collective-permute-start | bytes 196616 | tf_op jit(solution)/shard_map/while/body/eval_jaxpr/ppermute | solution.py:18
  892.2 13.3 %collective-permute-start.1 = (bf16[2,128,128]{2,1,0:T(8,128)(2,1)S(1)}, bf16[2,128,128]{2,1,0:T(8,128)(2,1)S(1)}, u32[]{:S(2)}, u32[]{:S(2)}) collective-permute-start(bf16[2,128,128]{2,1,0:T(8,128)(2,1)S(1)} %get-tuple-element.332), channel_id=1, source_target_pairs={{0,8},{8,16},{16,24},{24,32},{32,40},{40,48},{48,56},{56,64},{64,7... | collective-permute-start | bytes 196616 | tf_op jit(solution)/shard_map/while/body/eval_jaxpr/ppermute | solution.py:18
  906.2 13.3 %collective-permute-start.1 = (bf16[2,128,128]{2,1,0:T(8,128)(2,1)S(1)}, bf16[2,128,128]{2,1,0:T(8,128)(2,1)S(1)}, u32[]{:S(2)}, u32[]{:S(2)}) collective-permute-start(bf16[2,128,128]{2,1,0:T(8,128)(2,1)S(1)} %get-tuple-element.332), channel_id=1, source_target_pairs={{0,8},{8,16},{16,24},{24,32},{32,40},{40,48},{48,56},{56,64},{64,7... | collective-permute-start | bytes 196616 | tf_op jit(solution)/shard_map/while/body/eval_jaxpr/ppermute | solution.py:18
  920.1 13.3 %collective-permute-start.1 = (bf16[2,128,128]{2,1,0:T(8,128)(2,1)S(1)}, bf16[2,128,128]{2,1,0:T(8,128)(2,1)S(1)}, u32[]{:S(2)}, u32[]{:S(2)}) collective-permute-start(bf16[2,128,128]{2,1,0:T(8,128)(2,1)S(1)} %get-tuple-element.332), channel_id=1, source_target_pairs={{0,8},{8,16},{16,24},{24,32},{32,40},{40,48},{48,56},{56,64},{64,7... | collective-permute-start | bytes 196616 | tf_op jit(solution)/shard_map/while/body/eval_jaxpr/ppermute | solution.py:18
  934.1 13.3 %collective-permute-start.1 = (bf16[2,128,128]{2,1,0:T(8,128)(2,1)S(1)}, bf16[2,128,128]{2,1,0:T(8,128)(2,1)S(1)}, u32[]{:S(2)}, u32[]{:S(2)}) collective-permute-start(bf16[2,128,128]{2,1,0:T(8,128)(2,1)S(1)} %get-tuple-element.332), channel_id=1, source_target_pairs={{0,8},{8,16},{16,24},{24,32},{32,40},{40,48},{48,56},{56,64},{64,7... | collective-permute-start | bytes 196616 | tf_op jit(solution)/shard_map/while/body/eval_jaxpr/ppermute | solution.py:18
  948.0 13.3 %collective-permute-start.1 = (bf16[2,128,128]{2,1,0:T(8,128)(2,1)S(1)}, bf16[2,128,128]{2,1,0:T(8,128)(2,1)S(1)}, u32[]{:S(2)}, u32[]{:S(2)}) collective-permute-start(bf16[2,128,128]{2,1,0:T(8,128)(2,1)S(1)} %get-tuple-element.332), channel_id=1, source_target_pairs={{0,8},{8,16},{16,24},{24,32},{32,40},{40,48},{48,56},{56,64},{64,7... | collective-permute-start | bytes 196616 | tf_op jit(solution)/shard_map/while/body/eval_jaxpr/ppermute | solution.py:18
  962.0 13.3 %collective-permute-start.1 = (bf16[2,128,128]{2,1,0:T(8,128)(2,1)S(1)}, bf16[2,128,128]{2,1,0:T(8,128)(2,1)S(1)}, u32[]{:S(2)}, u32[]{:S(2)}) collective-permute-start(bf16[2,128,128]{2,1,0:T(8,128)(2,1)S(1)} %get-tuple-element.332), channel_id=1, source_target_pairs={{0,8},{8,16},{16,24},{24,32},{32,40},{40,48},{48,56},{56,64},{64,7... | collective-permute-start | bytes 196616 | tf_op jit(solution)/shard_map/while/body/eval_jaxpr/ppermute | solution.py:18
  976.0 13.3 %collective-permute-start.1 = (bf16[2,128,128]{2,1,0:T(8,128)(2,1)S(1)}, bf16[2,128,128]{2,1,0:T(8,128)(2,1)S(1)}, u32[]{:S(2)}, u32[]{:S(2)}) collective-permute-start(bf16[2,128,128]{2,1,0:T(8,128)(2,1)S(1)} %get-tuple-element.332), channel_id=1, source_target_pairs={{0,8},{8,16},{16,24},{24,32},{32,40},{40,48},{48,56},{56,64},{64,7... | collective-permute-start | bytes 196616 | tf_op jit(solution)/shard_map/while/body/eval_jaxpr/ppermute | solution.py:18
  989.9 13.3 %collective-permute-start.1 = (bf16[2,128,128]{2,1,0:T(8,128)(2,1)S(1)}, bf16[2,128,128]{2,1,0:T(8,128)(2,1)S(1)}, u32[]{:S(2)}, u32[]{:S(2)}) collective-permute-start(bf16[2,128,128]{2,1,0:T(8,128)(2,1)S(1)} %get-tuple-element.332), channel_id=1, source_target_pairs={{0,8},{8,16},{16,24},{24,32},{32,40},{40,48},{48,56},{56,64},{64,7... | collective-permute-start | bytes 196616 | tf_op jit(solution)/shard_map/while/body/eval_jaxpr/ppermute | solution.py:18
  1003.9 13.3 %collective-permute-start.1 = (bf16[2,128,128]{2,1,0:T(8,128)(2,1)S(1)}, bf16[2,128,128]{2,1,0:T(8,128)(2,1)S(1)}, u32[]{:S(2)}, u32[]{:S(2)}) collective-permute-start(bf16[2,128,128]{2,1,0:T(8,128)(2,1)S(1)} %get-tuple-element.332), channel_id=1, source_target_pairs={{0,8},{8,16},{16,24},{24,32},{32,40},{40,48},{48,56},{56,64},{64,7... | collective-permute-start | bytes 196616 | tf_op jit(solution)/shard_map/while/body/eval_jaxpr/ppermute | solution.py:18
  (70 other events, 2319.0 us)
Sparse Core Ops, SparseCore 0:
  9.4 69.9 all-gather.1
